TPU v7x, 256 devices: a whole 4x4x8 slice. The times are simulated.
256 devices in a mesh: segment: 4 (over z_lo), expert: 64 (over x, y, z_hi, core).
Axes of the slice: x: 4, y: 4, z: 8 (z_hi: 2, z_lo: 4; z = z_hi * 4 + z_lo), core: 2. Of those that a mesh axis runs over, the one named last changes fastest.
Arguments:
- forward_input: bfloat16 [4, 512, 7168], P('segment', 'expert'), may hold values from -6 to 6
- forward_routes: int32 [4, 512, 8], P('segment', 'expert'), may hold values from 0 to 15, all different within a row; in each aligned block of 8 rows (0 to 7, 8 to 15, ..., all dimensions but the last counted through in order) at most 8 rows name the same one
- forward_gates: float32 [4, 512, 8], P('segment', 'expert'), may hold values from 0.05 to 0.8
- gate_matrix: bfloat16 [4, 64, 7168, 256], P('segment', 'expert'), may hold values from -0.0625 to 0.0625
- up_matrix: bfloat16 [4, 64, 7168, 256], P('segment', 'expert'), may hold values from -0.0625 to 0.0625
- down_matrix: bfloat16 [4, 64, 256, 7168], P('segment', 'expert'), may hold values from -0.1875 to 0.1875
Outputs:
- next_input: bfloat16 [4, 512, 7168], P('segment', 'expert')
Inputs may be any that keep to these rules, and one draw needn't show every extreme that they name: `forward_routes`: each token names 8 different experts. Among the 8 tokens of one index of expert, no expert is named by more than 8 of them, and in every draw some expert is named by exactly 8 tokens of some index.
All inputs are finite; a program needn't handle non-finite values.
Results may differ from a plain program's by a relative error of at most 0.0065.
Values may be sent and summed in bfloat16 or wider, within the bound.
No kernel may reach another device: no remote copies, remote signals or barrier semaphores. Data moves between devices by JAX's collectives and lax.ppermute only.
A program may use at most 128 MiB of HBM per device.

v0:
```python
import jax
import jax.numpy as jnp
from jax import lax
from jax.sharding import PartitionSpec as P

FH = 1024
X_SIZE, Y_SIZE, Z_SIZE, C_SIZE = 4, 4, 2, 2


def coords(e):
    return (e // (Y_SIZE * Z_SIZE * C_SIZE), (e // (Z_SIZE * C_SIZE)) % Y_SIZE, (e // C_SIZE) % Z_SIZE, e % C_SIZE)


def index_of(x, y, z, c):
    return ((x * Y_SIZE + y) * Z_SIZE + z) * C_SIZE + c


def moved(value, target):
    count = X_SIZE * Y_SIZE * Z_SIZE * C_SIZE
    pairs = [(e, target(*coords(e))) for e in range(count)]
    return lax.ppermute(value, "expert", pairs)


def along(axis, step):
    def target(x, y, z, c):
        first = axis if c == 0 else 1 - axis
        if first == 0:
            return index_of((x + step) % X_SIZE, y, z, c)
        return index_of(x, (y + step) % Y_SIZE, z, c)

    return target


def across_z(x, y, z, c):
    return index_of(x, y, 1 - z, c)


def across_core(x, y, z, c):
    return index_of(x, y, z, 1 - c)


def expert_rows(rows, weight, gate_mat, upper_mat, down_mat):
    gate_act = jnp.dot(rows, gate_mat, preferred_element_type=jnp.float32)
    upper_act = jnp.dot(rows, upper_mat, preferred_element_type=jnp.float32)
    hidden = (jax.nn.silu(gate_act) * upper_act).astype(jnp.bfloat16)
    part = jnp.dot(hidden, down_mat, preferred_element_type=jnp.float32)
    return weight[:, None] * part.astype(jnp.bfloat16).astype(jnp.float32)


def coded(coef):
    first = coef.astype(jnp.bfloat16)
    rest = coef - first.astype(jnp.float32)
    second = rest.astype(jnp.bfloat16)
    third = (rest - second.astype(jnp.float32)).astype(jnp.bfloat16)
    return jnp.concatenate([first, second, third], axis=-1)


def decoded(code, groups):
    code = code.astype(jnp.float32)
    return code[..., :groups] + code[..., groups:2 * groups] + code[..., 2 * groups:3 * groups]


def layer(forward_input, forward_routes, forward_gates, gate_matrix, up_matrix, down_matrix):
    devices = lax.axis_size("expert")
    hidden_slice = gate_matrix.shape[3]
    split = FH // hidden_slice
    groups = devices // split
    tokens = forward_input[0]
    width = tokens.shape[1]
    me = lax.axis_index("expert")
    expert = me % groups
    named = forward_routes[0][:, :, None] == jnp.arange(groups, dtype=jnp.int32)[None, None, :]
    coef = jnp.sum(jnp.where(named, forward_gates[0][:, :, None], 0.0), axis=1)
    code = coded(coef)
    pad = 128 * ((code.shape[1] + 127) // 128) - code.shape[1]
    code = jnp.pad(code, ((0, 0), (0, pad)))
    col = jnp.concatenate([tokens, code], axis=1)

    mats = (
        jnp.pad(gate_matrix[0, 0], ((0, code.shape[1]), (0, 0))),
        jnp.pad(up_matrix[0, 0], ((0, code.shape[1]), (0, 0))),
        down_matrix[0, 0],
    )
    full = width + code.shape[1]
    ring = X_SIZE

    def served(block):
        first = jnp.stack([block] + [moved(block, along(0, k)) for k in range(1, ring)])
        second = jnp.stack([first] + [moved(first, along(1, k)) for k in range(1, ring)])
        other = moved(second, across_core)
        rows = jnp.stack([other, second]).reshape(-1, full)
        weight = decoded(rows[:, width:], groups)[:, expert]
        part = expert_rows(rows, weight, *mats).astype(jnp.bfloat16)
        half = part.shape[0] // 2
        back = moved(part[:half], across_core)
        summed = part[half:].astype(jnp.float32) + back.astype(jnp.float32)
        summed = summed.reshape((ring, ring) + tokens.shape)
        total = summed[0]
        sent = summed.astype(jnp.bfloat16)
        for m in range(1, ring):
            total = total + moved(sent[m], along(1, -m)).astype(jnp.float32)
        result = total[0]
        sent = total.astype(jnp.bfloat16)
        for k in range(1, ring):
            result = result + moved(sent[k], along(0, -k)).astype(jnp.float32)
        return result

    own_sum = served(col)
    partner_sum = served(moved(col, across_z))

    mine = tokens.astype(jnp.float32) + own_sum
    theirs = partner_sum.astype(jnp.bfloat16)
    sections = lax.axis_size("segment")
    count = X_SIZE * Y_SIZE * Z_SIZE * C_SIZE
    relay = [(s * count + e, (s + 1) % sections * count + e) for s in range(sections) for e in range(count)]
    cross = [
        (s * count + e, (s + 1) % sections * count + across_z(*coords(e)))
        for s in range(sections)
        for e in range(count)
    ]
    got_mine = lax.ppermute(mine, ("segment", "expert"), relay)
    got_theirs = lax.ppermute(theirs, ("segment", "expert"), cross)
    next_input = (got_mine + got_theirs.astype(jnp.float32)).astype(jnp.bfloat16)
    return next_input[None]


def solution(mesh):
    in_specs = (
        P("segment", "expert", None),
        P("segment", "expert", None),
        P("segment", "expert", None),
        P("segment", "expert", None, None),
        P("segment", "expert", None, None),
        P("segment", "expert", None, None),
    )
    out_specs = P("segment", "expert", None)
    return jax.shard_map(layer, mesh=mesh, in_specs=in_specs, out_specs=out_specs, check_vma=False)
```

profile of v0, /device:TPU:32, one launch (start us, length us, event | category | flops | bytes accessed | tf_op | source)
XLA Modules:
  0.0 147.9 jit_solution(15574317656670264296)
XLA Ops:
  0.9 0.9 fusion.59
  1.8 1.6 %collective-permute-start = (bf16[8,7296]{1,0:T(8,128)(2,1)S(1)}, bf16[8,7296]{1,0:T(8,128)(2,1)S(1)}, u32[]{:S(2)}, u32[]{:S(2)}) collective-permute-start(bf16[8,7296]{1,0:T(8,128)(2,1)S(1)} %get-tuple-element.34), channel_id=1, source_target_pairs={{0,16},{1,5},{2,18},{3,7},{4,20},{5,9},{6,22},{7,11},{8,24},{9,13}... | collective-permute-start | bytes 350216 | tf_op jit(solution)/shard_map/ppermute | solution.py:21
  3.4 2.7 %collective-permute-start.1 = (bf16[8,7296]{1,0:T(8,128)(2,1)S(1)}, bf16[8,7296]{1,0:T(8,128)(2,1)S(1)}, u32[]{:S(2)}, u32[]{:S(2)}) collective-permute-start(bf16[8,7296]{1,0:T(8,128)(2,1)S(1)} %get-tuple-element.34), channel_id=1, source_target_pairs={{0,32},{1,9},{2,34},{3,11},{4,36},{5,13},{6,38},{7,15},{8,40},{9,1... | collective-permute-start | bytes 350216 | tf_op jit(solution)/shard_map/ppermute | solution.py:21
  6.1 1.4 collective-permute-start.2
  7.9 2.2 %collective-permute-done.1 = bf16[8,7296]{1,0:T(8,128)(2,1)S(1)} collective-permute-done((bf16[8,7296]{1,0:T(8,128)(2,1)S(1)}, bf16[8,7296]{1,0:T(8,128)(2,1)S(1)}, u32[]{:S(2)}, u32[]{:S(2)}) %collective-permute-start.1) | collective-permute-done | bytes 116768 | tf_op jit(solution)/shard_map/ppermute | solution.py:21
  11.0 3.1 %collective-permute-start.5 = (bf16[4,8,7296]{2,1,0:T(8,128)(2,1)S(1)}, bf16[4,8,7296]{2,1,0:T(8,128)(2,1)S(1)}, u32[]{:S(2)}, u32[]{:S(2)}) collective-permute-start(bf16[4,8,7296]{2,1,0:T(8,128)(2,1)S(1)} %get-tuple-element.26), channel_id=1, source_target_pairs={{0,12},{1,49},{2,14},{3,51},{4,0},{5,53},{6,2},{7,55},{8,4},{9,57}... | collective-permute-start | bytes 1400840 | tf_op jit(solution)/shard_map/ppermute | solution.py:21
  14.1 2.2 %collective-permute-start.4 = (bf16[4,8,7296]{2,1,0:T(8,128)(2,1)S(1)}, bf16[4,8,7296]{2,1,0:T(8,128)(2,1)S(1)}, u32[]{:S(2)}, u32[]{:S(2)}) collective-permute-start(bf16[4,8,7296]{2,1,0:T(8,128)(2,1)S(1)} %get-tuple-element.26), channel_id=1, source_target_pairs={{0,8},{1,33},{2,10},{3,35},{4,12},{5,37},{6,14},{7,39},{8,0},{9,41... | collective-permute-start | bytes 1400840 | tf_op jit(solution)/shard_map/ppermute | solution.py:21
  16.3 6.3 %collective-permute-start.15 = (bf16[8,7296]{1,0:T(8,128)(2,1)S(1)}, bf16[8,7296]{1,0:T(8,128)(2,1)S(1)}, u32[]{:S(2)}, u32[]{:S(2)}) collective-permute-start(bf16[8,7296]{1,0:T(8,128)(2,1)S(1)} %get-tuple-element.34), channel_id=1, source_target_pairs={{0,2},{1,3},{2,0},{3,1},{4,6},{5,7},{6,4},{7,5},{8,10},{9,11},{10,... | collective-permute-start | bytes 350216 | tf_op jit(solution)/shard_map/ppermute | solution.py:21
  22.6 3.1 %collective-permute-done.15 = bf16[8,7296]{1,0:T(8,128)(2,1)S(1)} collective-permute-done((bf16[8,7296]{1,0:T(8,128)(2,1)S(1)}, bf16[8,7296]{1,0:T(8,128)(2,1)S(1)}, u32[]{:S(2)}, u32[]{:S(2)}) %collective-permute-start.15) | collective-permute-done | bytes 116768 | tf_op jit(solution)/shard_map/ppermute | solution.py:21
  25.7 1.6 %collective-permute-start.16 = (bf16[8,7296]{1,0:T(8,128)(2,1)S(1)}, bf16[8,7296]{1,0:T(8,128)(2,1)S(1)}, u32[]{:S(2)}, u32[]{:S(2)}) collective-permute-start(bf16[8,7296]{1,0:T(8,128)(2,1)S(1)} %collective-permute-done.15), channel_id=1, source_target_pairs={{0,16},{1,5},{2,18},{3,7},{4,20},{5,9},{6,22},{7,11},{8,24},{9,13}... | collective-permute-start | bytes 350216 | tf_op jit(solution)/shard_map/ppermute | solution.py:21
  27.2 3.1 %collective-permute-start.17 = (bf16[8,7296]{1,0:T(8,128)(2,1)S(1)}, bf16[8,7296]{1,0:T(8,128)(2,1)S(1)}, u32[]{:S(2)}, u32[]{:S(2)}) collective-permute-start(bf16[8,7296]{1,0:T(8,128)(2,1)S(1)} %collective-permute-done.15), channel_id=1, source_target_pairs={{0,32},{1,9},{2,34},{3,11},{4,36},{5,13},{6,38},{7,15},{8,40},{9,1... | collective-permute-start | bytes 350216 | tf_op jit(solution)/shard_map/ppermute | solution.py:21
  31.1 1.6 %pad_maximum_fusion.2 = (bf16[4,4,8,7296]{3,2,1,0:T(8,128)(2,1)}, bf16[1,4,4,8,7296]{4,3,2,1,0:T(8,128)(2,1)S(1)}) fusion(bf16[1,4,8,7296]{3,2,1,0:T(8,128)(2,1)S(1)} %bitcast.114, bf16[1,4,8,7296]{3,2,1,0:T(8,128)(2,1)S(1)} %bitcast.116, bf16[1,4,8,7296]{3,2,1,0:T(8,128)(2,1)S(1)} %bitcast.115, bf16[1,4,8,7296]{3,2,1,0:T(8,128)(2,1)S(1)} %get-tuple-element.25), kind=kLoop, calls=%fused_computation.22 | loop fusion | flops 2801664 | bytes 5603328 | tf_op jit(solution)/shard_map/stack | solution.py:89
  32.7 1.7 %collective-permute-done.17 = bf16[8,7296]{1,0:T(8,128)(2,1)S(1)} collective-permute-done((bf16[8,7296]{1,0:T(8,128)(2,1)S(1)}, bf16[8,7296]{1,0:T(8,128)(2,1)S(1)}, u32[]{:S(2)}, u32[]{:S(2)}) %collective-permute-start.17) | collective-permute-done | bytes 116768 | tf_op jit(solution)/shard_map/ppermute | solution.py:21
  35.2 2.0 %collective-permute-start.19 = (bf16[4,8,7296]{2,1,0:T(8,128)(2,1)S(1)}, bf16[4,8,7296]{2,1,0:T(8,128)(2,1)S(1)}, u32[]{:S(2)}, u32[]{:S(2)}) collective-permute-start(bf16[4,8,7296]{2,1,0:T(8,128)(2,1)S(1)} %get-tuple-element.24), channel_id=1, source_target_pairs={{0,4},{1,17},{2,6},{3,19},{4,8},{5,21},{6,10},{7,23},{8,12},{9,25}... | collective-permute-start | bytes 1400840 | tf_op jit(solution)/shard_map/ppermute | solution.py:21
  37.2 1.4 collective-permute-start.20
  38.6 1.3 collective-permute-start.21
  40.0 5.1 %collective-permute-done.19 = bf16[4,8,7296]{2,1,0:T(8,128)(2,1)S(1)} collective-permute-done((bf16[4,8,7296]{2,1,0:T(8,128)(2,1)S(1)}, bf16[4,8,7296]{2,1,0:T(8,128)(2,1)S(1)}, u32[]{:S(2)}, u32[]{:S(2)}) %collective-permute-start.19) | collective-permute-done | bytes 466976 | tf_op jit(solution)/shard_map/ppermute | solution.py:21
  45.1 5.1 %collective-permute-done.20 = bf16[4,8,7296]{2,1,0:T(8,128)(2,1)S(1)} collective-permute-done((bf16[4,8,7296]{2,1,0:T(8,128)(2,1)S(1)}, bf16[4,8,7296]{2,1,0:T(8,128)(2,1)S(1)}, u32[]{:S(2)}, u32[]{:S(2)}) %collective-permute-start.20) | collective-permute-done | bytes 466976 | tf_op jit(solution)/shard_map/ppermute | solution.py:21
  51.0 2.2 %pad_maximum_fusion.3 = (bf16[4,4,8,7296]{3,2,1,0:T(8,128)(2,1)}, bf16[1,4,4,8,7296]{4,3,2,1,0:T(8,128)(2,1)}) fusion(bf16[1,4,8,7296]{3,2,1,0:T(8,128)(2,1)S(1)} %bitcast.119, bf16[1,4,8,7296]{3,2,1,0:T(8,128)(2,1)S(1)} %bitcast.118, bf16[1,4,8,7296]{3,2,1,0:T(8,128)(2,1)S(1)} %bitcast.117, bf16[1,4,8,7296]{3,2,1,0:T(8,128)(2,1)S(1)} %get-tuple-element.23), kind=kLoop, calls=%fused_computation.23 | loop fusion | flops 2801664 | bytes 5603328 | tf_op jit(solution)/shard_map/stack | solution.py:89
  53.2 1.9 %pad_maximum_fusion = bf16[2,4,4,8,7296]{4,3,2,1,0:T(8,128)(2,1)S(1)} fusion(bf16[1,4,4,8,7296]{4,3,2,1,0:T(8,128)(2,1)S(1)} %get-tuple-element.16, bf16[1,4,4,8,7296]{4,3,2,1,0:T(8,128)(2,1)} %bitcast.11), kind=kLoop, calls=%fused_computation.8 | loop fusion | flops 1867776 | bytes 7471104 | tf_op jit(solution)/shard_map/stack | solution.py:91
  55.1 1.8 %copy-done.1 = bf16[2,4,4,8,7296]{4,3,2,1,0:T(8,128)(2,1)} copy-done((bf16[2,4,4,8,7296]{4,3,2,1,0:T(8,128)(2,1)}, bf16[2,4,4,8,7296]{4,3,2,1,0:T(8,128)(2,1)S(1)}, u32[]{:S(2)}) %copy-start.1) | copy-done | bytes 3735576
  57.0 4.4 %fusion.10 = f32[256,256]{1,0:T(8,128)S(1)} fusion(bf16[256,7296]{1,0:T(8,128)(2,1)} %bitcast.109, bf16[7168,256]{1,0:T(8,128)(2,1)} %bitcast.132), kind=kOutput, calls=%fused_computation.16 | convolution fusion | flops 956301312 | bytes 7667712 | tf_op jit(solution)/shard_map/dot_general | solution.py:44
  61.5 1.9 %pad_maximum_fusion.1 = bf16[2,4,4,8,7296]{4,3,2,1,0:T(8,128)(2,1)S(1)} fusion(bf16[1,4,4,8,7296]{4,3,2,1,0:T(8,128)(2,1)S(1)} %copy-done, bf16[1,4,4,8,7296]{4,3,2,1,0:T(8,128)(2,1)} %bitcast.34), kind=kLoop, calls=%fused_computation.9 | loop fusion | flops 1867776 | bytes 7471104 | tf_op jit(solution)/shard_map/stack | solution.py:91
  63.4 1.8 %copy-done.2 = bf16[2,4,4,8,7296]{4,3,2,1,0:T(8,128)(2,1)} copy-done((bf16[2,4,4,8,7296]{4,3,2,1,0:T(8,128)(2,1)}, bf16[2,4,4,8,7296]{4,3,2,1,0:T(8,128)(2,1)S(1)}, u32[]{:S(2)}) %copy-start.2) | copy-done | bytes 3735576
  65.4 10.1 %fusion.5 = bf16[256,7168]{1,0:T(8,128)(2,1)} fusion(bf16[1,1,256,7168]{3,2,1,0:T(8,128)(2,1)} %param.11, f32[256]{0:T(256)S(1)} %bitcast.131, f32[256,256]{1,0:T(8,128)S(1)} %fusion.10, bf16[256,7296]{1,0:T(8,128)(2,1)} %bitcast.110, bf16[7168,256]{1,0:T(8,128)(2,1)} %bitcast.134), kind=kOutput, calls=%fused_computation.7 | convolution fusion | flops 1903558656 | bytes 15008768 | tf_op jit(solution)/shard_map/dot_general | solution.py:46
  75.5 1.6 %slice.125 = bf16[128,7168]{1,0:T(8,128)(2,1)S(1)} slice(bf16[256,7168]{1,0:T(8,128)(2,1)} %fusion.5), slice={[0:128], [0:7168]} | slice | bytes 3670016 | tf_op jit(solution)/shard_map/slice | solution.py:95
  77.7 4.3 %fusion.8 = f32[256,256]{1,0:T(8,128)S(1)} fusion(bf16[256,7296]{1,0:T(8,128)(2,1)} %bitcast.112, bf16[7168,256]{1,0:T(8,128)(2,1)} %bitcast.133), kind=kOutput, calls=%fused_computation.14 | convolution fusion | flops 956301312 | bytes 7667712 | tf_op jit(solution)/shard_map/dot_general | solution.py:44
  82.0 10.0 %fusion.2 = bf16[256,7168]{1,0:T(8,128)(2,1)} fusion(bf16[1,1,256,7168]{3,2,1,0:T(8,128)(2,1)} %param.11, f32[256]{0:T(256)S(1)} %bitcast.130, f32[256,256]{1,0:T(8,128)S(1)} %fusion.8, bf16[256,7296]{1,0:T(8,128)(2,1)} %bitcast.113, bf16[7168,256]{1,0:T(8,128)(2,1)} %bitcast.135), kind=kOutput, calls=%fused_computation.3 | convolution fusion | flops 1903558656 | bytes 15008768 | tf_op jit(solution)/shard_map/dot_general | solution.py:46
  92.0 1.8 %slice.139 = bf16[128,7168]{1,0:T(8,128)(2,1)S(1)} slice(bf16[256,7168]{1,0:T(8,128)(2,1)} %fusion.2), slice={[0:128], [0:7168]} | slice | bytes 3670016 | tf_op jit(solution)/shard_map/slice | solution.py:95
  94.6 2.2 %convert_add_fusion.1 = (f32[128,7168]{1,0:T(8,128)S(1)}, bf16[128,7168]{1,0:T(8,128)(2,1)S(1)}) fusion(bf16[128,7168]{1,0:T(8,128)(2,1)} %collective-permute-done.7, bf16[256,7168]{1,0:T(8,128)(2,1)S(1)} %copy-done.4), kind=kLoop, calls=%fused_computation.13 | loop fusion | flops 3670016 | bytes 9175040 | tf_op jit(solution)/shard_map/add | solution.py:96
  96.9 1.5 collective-permute-start.10
  98.4 1.9 %collective-permute-start.8 = (bf16[4,8,7168]{2,1,0:T(8,128)(2,1)S(1)}, bf16[4,8,7168]{2,1,0:T(8,128)(2,1)S(1)}, u32[]{:S(2)}, u32[]{:S(2)}) collective-permute-start(bf16[4,8,7168]{2,1,0:T(8,128)(2,1)S(1)} %get-tuple-element.20), channel_id=1, source_target_pairs={{0,12},{1,49},{2,14},{3,51},{4,0},{5,53},{6,2},{7,55},{8,4},{9,57}... | collective-permute-start | bytes 1376264 | tf_op jit(solution)/shard_map/ppermute | solution.py:21
  100.2 0.9 collective-permute-start.9
  101.7 2.1 %collective-permute-start.24 = (bf16[4,8,7168]{2,1,0:T(8,128)(2,1)S(1)}, bf16[4,8,7168]{2,1,0:T(8,128)(2,1)S(1)}, u32[]{:S(2)}, u32[]{:S(2)}) collective-permute-start(bf16[4,8,7168]{2,1,0:T(8,128)(2,1)S(1)} %get-tuple-element.17), channel_id=1, source_target_pairs={{0,12},{1,49},{2,14},{3,51},{4,0},{5,53},{6,2},{7,55},{8,4},{9,57}... | collective-permute-start | bytes 1376264 | tf_op jit(solution)/shard_map/ppermute | solution.py:21
  103.8 1.5 %collective-permute-start.25 = (bf16[4,8,7168]{2,1,0:T(8,128)(2,1)S(1)}, bf16[4,8,7168]{2,1,0:T(8,128)(2,1)S(1)}, u32[]{:S(2)}, u32[]{:S(2)}) collective-permute-start(bf16[4,8,7168]{2,1,0:T(8,128)(2,1)S(1)} %get-tuple-element.19), channel_id=1, source_target_pairs={{0,8},{1,33},{2,10},{3,35},{4,12},{5,37},{6,14},{7,39},{8,0},{9,41... | collective-permute-start | bytes 1376264 | tf_op jit(solution)/shard_map/ppermute | solution.py:21
  105.3 1.4 collective-permute-done.10
  106.8 4.3 %collective-permute-done.8 = bf16[4,8,7168]{2,1,0:T(8,128)(2,1)S(1)} collective-permute-done((bf16[4,8,7168]{2,1,0:T(8,128)(2,1)S(1)}, bf16[4,8,7168]{2,1,0:T(8,128)(2,1)S(1)}, u32[]{:S(2)}, u32[]{:S(2)}) %collective-permute-start.8) | collective-permute-done | bytes 458784 | tf_op jit(solution)/shard_map/ppermute | solution.py:21
  111.2 1.4 collective-permute-done.9
  112.8 2.0 %collective-permute-start.11 = (bf16[8,7168]{1,0:T(8,128)(2,1)S(1)}, bf16[8,7168]{1,0:T(8,128)(2,1)S(1)}, u32[]{:S(2)}, u32[]{:S(2)}) collective-permute-start(bf16[8,7168]{1,0:T(8,128)(2,1)S(1)} %get-tuple-element.30), channel_id=1, source_target_pairs={{0,48},{1,13},{2,50},{3,15},{4,52},{5,1},{6,54},{7,3},{8,56},{9,5}... | collective-permute-start | bytes 344072 | tf_op jit(solution)/shard_map/ppermute | solution.py:21
  114.8 0.9 collective-permute-start.12
  115.6 7.8 %collective-permute-done.24 = bf16[4,8,7168]{2,1,0:T(8,128)(2,1)S(1)} collective-permute-done((bf16[4,8,7168]{2,1,0:T(8,128)(2,1)S(1)}, bf16[4,8,7168]{2,1,0:T(8,128)(2,1)S(1)}, u32[]{:S(2)}, u32[]{:S(2)}) %collective-permute-start.24) | collective-permute-done | bytes 458784 | tf_op jit(solution)/shard_map/ppermute | solution.py:21
  124.4 2.6 %collective-permute-start.27 = (bf16[8,7168]{1,0:T(8,128)(2,1)S(1)}, bf16[8,7168]{1,0:T(8,128)(2,1)S(1)}, u32[]{:S(2)}, u32[]{:S(2)}) collective-permute-start(bf16[8,7168]{1,0:T(8,128)(2,1)S(1)} %get-tuple-element.27), channel_id=1, source_target_pairs={{0,48},{1,13},{2,50},{3,15},{4,52},{5,1},{6,54},{7,3},{8,56},{9,5}... | collective-permute-start | bytes 344072 | tf_op jit(solution)/shard_map/ppermute | solution.py:21
  128.0 1.5 collective-permute-done.13
  129.5 2.1 %collective-permute-start.14 = (f32[8,7168]{1,0:T(8,128)S(1)}, f32[8,7168]{1,0:T(8,128)S(1)}, u32[]{:S(2)}, u32[]{:S(2)}) collective-permute-start(f32[8,7168]{1,0:T(8,128)S(1)} %fusion.29), channel_id=1, source_target_pairs={{0,64},{1,65},{2,66},{3,67},{4,68},{5,69},{6,70},{7,71},{8,72},{9,... | collective-permute-start | bytes 688136 | tf_op jit(solution)/shard_map/ppermute | solution.py:121
  131.7 1.7 %collective-permute-done.28 = bf16[8,7168]{1,0:T(8,128)(2,1)S(1)} collective-permute-done((bf16[8,7168]{1,0:T(8,128)(2,1)S(1)}, bf16[8,7168]{1,0:T(8,128)(2,1)S(1)}, u32[]{:S(2)}, u32[]{:S(2)}) %collective-permute-start.28) | collective-permute-done | bytes 114720 | tf_op jit(solution)/shard_map/ppermute | solution.py:21
  133.4 1.2 collective-permute-done.29
  134.6 4.7 %collective-permute-start.30 = (bf16[8,7168]{1,0:T(8,128)(2,1)S(1)}, bf16[8,7168]{1,0:T(8,128)(2,1)S(1)}, u32[]{:S(2)}, u32[]{:S(2)}) collective-permute-start(bf16[8,7168]{1,0:T(8,128)(2,1)S(1)} %fusion.25), channel_id=1, source_target_pairs={{0,66},{1,67},{2,64},{3,65},{4,70},{5,71},{6,68},{7,69},{8,74},{9,... | collective-permute-start | bytes 344072 | tf_op jit(solution)/shard_map/ppermute | solution.py:122
  139.3 7.9 %collective-permute-done.30 = bf16[8,7168]{1,0:T(8,128)(2,1)S(1)} collective-permute-done((bf16[8,7168]{1,0:T(8,128)(2,1)S(1)}, bf16[8,7168]{1,0:T(8,128)(2,1)S(1)}, u32[]{:S(2)}, u32[]{:S(2)}) %collective-permute-start.30) | collective-permute-done | bytes 114720 | tf_op jit(solution)/shard_map/ppermute | solution.py:122
  (60 shorter events, 10.0 us)
Async XLA Ops:
  1.8 6.1 %collective-permute-start = (bf16[8,7296]{1,0:T(8,128)(2,1)S(1)}, bf16[8,7296]{1,0:T(8,128)(2,1)S(1)}, u32[]{:S(2)}, u32[]{:S(2)}) collective-permute-start(bf16[8,7296]{1,0:T(8,128)(2,1)S(1)} %get-tuple-element.34), channel_id=1, source_target_pairs={{0,16},{1,5},{2,18},{3,7},{4,20},{5,9},{6,22},{7,11},{8,24},{9,13}... | collective-permute-start | bytes 350216 | tf_op jit(solution)/shard_map/ppermute | solution.py:21
  3.4 6.8 %collective-permute-start.1 = (bf16[8,7296]{1,0:T(8,128)(2,1)S(1)}, bf16[8,7296]{1,0:T(8,128)(2,1)S(1)}, u32[]{:S(2)}, u32[]{:S(2)}) collective-permute-start(bf16[8,7296]{1,0:T(8,128)(2,1)S(1)} %get-tuple-element.34), channel_id=1, source_target_pairs={{0,32},{1,9},{2,34},{3,11},{4,36},{5,13},{6,38},{7,15},{8,40},{9,1... | collective-permute-start | bytes 350216 | tf_op jit(solution)/shard_map/ppermute | solution.py:21
  6.1 4.8 %collective-permute-start.2 = (bf16[8,7296]{1,0:T(8,128)(2,1)S(1)}, bf16[8,7296]{1,0:T(8,128)(2,1)S(1)}, u32[]{:S(2)}, u32[]{:S(2)}) collective-permute-start(bf16[8,7296]{1,0:T(8,128)(2,1)S(1)} %get-tuple-element.34), channel_id=1, source_target_pairs={{0,48},{1,13},{2,50},{3,15},{4,52},{5,1},{6,54},{7,3},{8,56},{9,5}... | collective-permute-start | bytes 350216 | tf_op jit(solution)/shard_map/ppermute | solution.py:21
  11.0 19.3 %collective-permute-start.5 = (bf16[4,8,7296]{2,1,0:T(8,128)(2,1)S(1)}, bf16[4,8,7296]{2,1,0:T(8,128)(2,1)S(1)}, u32[]{:S(2)}, u32[]{:S(2)}) collective-permute-start(bf16[4,8,7296]{2,1,0:T(8,128)(2,1)S(1)} %get-tuple-element.26), channel_id=1, source_target_pairs={{0,12},{1,49},{2,14},{3,51},{4,0},{5,53},{6,2},{7,55},{8,4},{9,57}... | collective-permute-start | bytes 1400840 | tf_op jit(solution)/shard_map/ppermute | solution.py:21
  14.1 17.0 %collective-permute-start.3 = (bf16[4,8,7296]{2,1,0:T(8,128)(2,1)S(1)}, bf16[4,8,7296]{2,1,0:T(8,128)(2,1)S(1)}, u32[]{:S(2)}, u32[]{:S(2)}) collective-permute-start(bf16[4,8,7296]{2,1,0:T(8,128)(2,1)S(1)} %get-tuple-element.26), channel_id=1, source_target_pairs={{0,4},{1,17},{2,6},{3,19},{4,8},{5,21},{6,10},{7,23},{8,12},{9,25}... | collective-permute-start | bytes 1400840 | tf_op jit(solution)/shard_map/ppermute | solution.py:21
  14.1 17.0 %collective-permute-start.4 = (bf16[4,8,7296]{2,1,0:T(8,128)(2,1)S(1)}, bf16[4,8,7296]{2,1,0:T(8,128)(2,1)S(1)}, u32[]{:S(2)}, u32[]{:S(2)}) collective-permute-start(bf16[4,8,7296]{2,1,0:T(8,128)(2,1)S(1)} %get-tuple-element.26), channel_id=1, source_target_pairs={{0,8},{1,33},{2,10},{3,35},{4,12},{5,37},{6,14},{7,39},{8,0},{9,41... | collective-permute-start | bytes 1400840 | tf_op jit(solution)/shard_map/ppermute | solution.py:21
  16.3 9.4 %collective-permute-start.15 = (bf16[8,7296]{1,0:T(8,128)(2,1)S(1)}, bf16[8,7296]{1,0:T(8,128)(2,1)S(1)}, u32[]{:S(2)}, u32[]{:S(2)}) collective-permute-start(bf16[8,7296]{1,0:T(8,128)(2,1)S(1)} %get-tuple-element.34), channel_id=1, source_target_pairs={{0,2},{1,3},{2,0},{3,1},{4,6},{5,7},{6,4},{7,5},{8,10},{9,11},{10,... | collective-permute-start | bytes 350216 | tf_op jit(solution)/shard_map/ppermute | solution.py:21
  25.7 7.0 %collective-permute-start.16 = (bf16[8,7296]{1,0:T(8,128)(2,1)S(1)}, bf16[8,7296]{1,0:T(8,128)(2,1)S(1)}, u32[]{:S(2)}, u32[]{:S(2)}) collective-permute-start(bf16[8,7296]{1,0:T(8,128)(2,1)S(1)} %collective-permute-done.15), channel_id=1, source_target_pairs={{0,16},{1,5},{2,18},{3,7},{4,20},{5,9},{6,22},{7,11},{8,24},{9,13}... | collective-permute-start | bytes 350216 | tf_op jit(solution)/shard_map/ppermute | solution.py:21
  27.2 7.1 %collective-permute-start.17 = (bf16[8,7296]{1,0:T(8,128)(2,1)S(1)}, bf16[8,7296]{1,0:T(8,128)(2,1)S(1)}, u32[]{:S(2)}, u32[]{:S(2)}) collective-permute-start(bf16[8,7296]{1,0:T(8,128)(2,1)S(1)} %collective-permute-done.15), channel_id=1, source_target_pairs={{0,32},{1,9},{2,34},{3,11},{4,36},{5,13},{6,38},{7,15},{8,40},{9,1... | collective-permute-start | bytes 350216 | tf_op jit(solution)/shard_map/ppermute | solution.py:21
  30.3 4.8 %collective-permute-start.18 = (bf16[8,7296]{1,0:T(8,128)(2,1)S(1)}, bf16[8,7296]{1,0:T(8,128)(2,1)S(1)}, u32[]{:S(2)}, u32[]{:S(2)}) collective-permute-start(bf16[8,7296]{1,0:T(8,128)(2,1)S(1)} %collective-permute-done.15), channel_id=1, source_target_pairs={{0,48},{1,13},{2,50},{3,15},{4,52},{5,1},{6,54},{7,3},{8,56},{9,5}... | collective-permute-start | bytes 350216 | tf_op jit(solution)/shard_map/ppermute | solution.py:21
  32.7 20.5 %collective-permute-start.6 = (bf16[4,4,8,7296]{3,2,1,0:T(8,128)(2,1)}, bf16[4,4,8,7296]{3,2,1,0:T(8,128)(2,1)}, u32[]{:S(2)}, u32[]{:S(2)}) collective-permute-start(bf16[4,4,8,7296]{3,2,1,0:T(8,128)(2,1)} %get-tuple-element.15), channel_id=1, source_target_pairs={{0,1},{1,0},{2,3},{3,2},{4,5},{5,4},{6,7},{7,6},{8,9},{9,8},{10,11... | collective-permute-start | bytes 5603336 | tf_op jit(solution)/shard_map/ppermute | solution.py:21
  35.2 9.9 %collective-permute-start.19 = (bf16[4,8,7296]{2,1,0:T(8,128)(2,1)S(1)}, bf16[4,8,7296]{2,1,0:T(8,128)(2,1)S(1)}, u32[]{:S(2)}, u32[]{:S(2)}) collective-permute-start(bf16[4,8,7296]{2,1,0:T(8,128)(2,1)S(1)} %get-tuple-element.24), channel_id=1, source_target_pairs={{0,4},{1,17},{2,6},{3,19},{4,8},{5,21},{6,10},{7,23},{8,12},{9,25}... | collective-permute-start | bytes 1400840 | tf_op jit(solution)/shard_map/ppermute | solution.py:21
  37.2 13.0 %collective-permute-start.20 = (bf16[4,8,7296]{2,1,0:T(8,128)(2,1)S(1)}, bf16[4,8,7296]{2,1,0:T(8,128)(2,1)S(1)}, u32[]{:S(2)}, u32[]{:S(2)}) collective-permute-start(bf16[4,8,7296]{2,1,0:T(8,128)(2,1)S(1)} %get-tuple-element.24), channel_id=1, source_target_pairs={{0,8},{1,33},{2,10},{3,35},{4,12},{5,37},{6,14},{7,39},{8,0},{9,41... | collective-permute-start | bytes 1400840 | tf_op jit(solution)/shard_map/ppermute | solution.py:21
  38.6 12.4 %collective-permute-start.21 = (bf16[4,8,7296]{2,1,0:T(8,128)(2,1)S(1)}, bf16[4,8,7296]{2,1,0:T(8,128)(2,1)S(1)}, u32[]{:S(2)}, u32[]{:S(2)}) collective-permute-start(bf16[4,8,7296]{2,1,0:T(8,128)(2,1)S(1)} %get-tuple-element.24), channel_id=1, source_target_pairs={{0,12},{1,49},{2,14},{3,51},{4,0},{5,53},{6,2},{7,55},{8,4},{9,57}... | collective-permute-start | bytes 1400840 | tf_op jit(solution)/shard_map/ppermute | solution.py:21
  53.1 8.3 %collective-permute-start.22 = (bf16[4,4,8,7296]{3,2,1,0:T(8,128)(2,1)}, bf16[4,4,8,7296]{3,2,1,0:T(8,128)(2,1)}, u32[]{:S(2)}, u32[]{:S(2)}) collective-permute-start(bf16[4,4,8,7296]{3,2,1,0:T(8,128)(2,1)} %get-tuple-element.13), channel_id=1, source_target_pairs={{0,1},{1,0},{2,3},{3,2},{4,5},{5,4},{6,7},{7,6},{8,9},{9,8},{10,11... | collective-permute-start | bytes 5603336 | tf_op jit(solution)/shard_map/ppermute | solution.py:21
  55.1 1.8 %copy-start.1 = (bf16[2,4,4,8,7296]{4,3,2,1,0:T(8,128)(2,1)}, bf16[2,4,4,8,7296]{4,3,2,1,0:T(8,128)(2,1)S(1)}, u32[]{:S(2)}) copy-start(bf16[2,4,4,8,7296]{4,3,2,1,0:T(8,128)(2,1)S(1)} %pad_maximum_fusion) | copy-start | bytes 11206660
  57.0 4.5 %copy-start = (bf16[1,4,4,8,7296]{4,3,2,1,0:T(8,128)(2,1)S(1)}, bf16[1,4,4,8,7296]{4,3,2,1,0:T(8,128)(2,1)}, u32[]{:S(2)}) copy-start(bf16[1,4,4,8,7296]{4,3,2,1,0:T(8,128)(2,1)} %get-tuple-element.14) | copy-start | bytes 5603332
  63.4 1.8 %copy-start.2 = (bf16[2,4,4,8,7296]{4,3,2,1,0:T(8,128)(2,1)}, bf16[2,4,4,8,7296]{4,3,2,1,0:T(8,128)(2,1)S(1)}, u32[]{:S(2)}) copy-start(bf16[2,4,4,8,7296]{4,3,2,1,0:T(8,128)(2,1)S(1)} %pad_maximum_fusion.1) | copy-start | bytes 11206660
  77.1 16.8 %collective-permute-start.7 = (bf16[128,7168]{1,0:T(8,128)(2,1)S(1)}, bf16[128,7168]{1,0:T(8,128)(2,1)}, u32[]{:S(2)}, u32[]{:S(2)}) collective-permute-start(bf16[128,7168]{1,0:T(8,128)(2,1)S(1)} %slice.125), channel_id=1, source_target_pairs={{0,1},{1,0},{2,3},{3,2},{4,5},{5,4},{6,7},{7,6},{8,9},{9,8},{10,11... | collective-permute-start | bytes 5505032 | tf_op jit(solution)/shard_map/ppermute | solution.py:21
  92.0 2.6 %copy-start.4 = (bf16[256,7168]{1,0:T(8,128)(2,1)S(1)}, bf16[256,7168]{1,0:T(8,128)(2,1)}, u32[]{:S(2)}) copy-start(bf16[256,7168]{1,0:T(8,128)(2,1)} %fusion.5) | copy-start | bytes 11010052
  93.8 7.3 %collective-permute-start.23 = (bf16[128,7168]{1,0:T(8,128)(2,1)S(1)}, bf16[128,7168]{1,0:T(8,128)(2,1)S(1)}, u32[]{:S(2)}, u32[]{:S(2)}) collective-permute-start(bf16[128,7168]{1,0:T(8,128)(2,1)S(1)} %slice.139), channel_id=1, source_target_pairs={{0,1},{1,0},{2,3},{3,2},{4,5},{5,4},{6,7},{7,6},{8,9},{9,8},{10,11... | collective-permute-start | bytes 5505032 | tf_op jit(solution)/shard_map/ppermute | solution.py:21
  94.6 6.5 %copy-start.3 = (bf16[256,7168]{1,0:T(8,128)(2,1)S(1)}, bf16[256,7168]{1,0:T(8,128)(2,1)}, u32[]{:S(2)}) copy-start(bf16[256,7168]{1,0:T(8,128)(2,1)} %fusion.2) | copy-start | bytes 11010052
  96.9 9.8 %collective-permute-start.10 = (bf16[4,8,7168]{2,1,0:T(8,128)(2,1)S(1)}, bf16[4,8,7168]{2,1,0:T(8,128)(2,1)S(1)}, u32[]{:S(2)}, u32[]{:S(2)}) collective-permute-start(bf16[4,8,7168]{2,1,0:T(8,128)(2,1)S(1)} %get-tuple-element.21), channel_id=1, source_target_pairs={{0,4},{1,17},{2,6},{3,19},{4,8},{5,21},{6,10},{7,23},{8,12},{9,25}... | collective-permute-start | bytes 1376264 | tf_op jit(solution)/shard_map/ppermute | solution.py:21
  98.4 12.8 %collective-permute-start.8 = (bf16[4,8,7168]{2,1,0:T(8,128)(2,1)S(1)}, bf16[4,8,7168]{2,1,0:T(8,128)(2,1)S(1)}, u32[]{:S(2)}, u32[]{:S(2)}) collective-permute-start(bf16[4,8,7168]{2,1,0:T(8,128)(2,1)S(1)} %get-tuple-element.20), channel_id=1, source_target_pairs={{0,12},{1,49},{2,14},{3,51},{4,0},{5,53},{6,2},{7,55},{8,4},{9,57}... | collective-permute-start | bytes 1376264 | tf_op jit(solution)/shard_map/ppermute | solution.py:21
  100.2 12.3 %collective-permute-start.9 = (bf16[4,8,7168]{2,1,0:T(8,128)(2,1)S(1)}, bf16[4,8,7168]{2,1,0:T(8,128)(2,1)S(1)}, u32[]{:S(2)}, u32[]{:S(2)}) collective-permute-start(bf16[4,8,7168]{2,1,0:T(8,128)(2,1)S(1)} %get-tuple-element.22), channel_id=1, source_target_pairs={{0,8},{1,33},{2,10},{3,35},{4,12},{5,37},{6,14},{7,39},{8,0},{9,41... | collective-permute-start | bytes 1376264 | tf_op jit(solution)/shard_map/ppermute | solution.py:21
  101.7 21.7 %collective-permute-start.24 = (bf16[4,8,7168]{2,1,0:T(8,128)(2,1)S(1)}, bf16[4,8,7168]{2,1,0:T(8,128)(2,1)S(1)}, u32[]{:S(2)}, u32[]{:S(2)}) collective-permute-start(bf16[4,8,7168]{2,1,0:T(8,128)(2,1)S(1)} %get-tuple-element.17), channel_id=1, source_target_pairs={{0,12},{1,49},{2,14},{3,51},{4,0},{5,53},{6,2},{7,55},{8,4},{9,57}... | collective-permute-start | bytes 1376264 | tf_op jit(solution)/shard_map/ppermute | solution.py:21
  103.8 20.4 %collective-permute-start.25 = (bf16[4,8,7168]{2,1,0:T(8,128)(2,1)S(1)}, bf16[4,8,7168]{2,1,0:T(8,128)(2,1)S(1)}, u32[]{:S(2)}, u32[]{:S(2)}) collective-permute-start(bf16[4,8,7168]{2,1,0:T(8,128)(2,1)S(1)} %get-tuple-element.19), channel_id=1, source_target_pairs={{0,8},{1,33},{2,10},{3,35},{4,12},{5,37},{6,14},{7,39},{8,0},{9,41... | collective-permute-start | bytes 1376264 | tf_op jit(solution)/shard_map/ppermute | solution.py:21
  106.7 17.5 %collective-permute-start.26 = (bf16[4,8,7168]{2,1,0:T(8,128)(2,1)S(1)}, bf16[4,8,7168]{2,1,0:T(8,128)(2,1)S(1)}, u32[]{:S(2)}, u32[]{:S(2)}) collective-permute-start(bf16[4,8,7168]{2,1,0:T(8,128)(2,1)S(1)} %get-tuple-element.18), channel_id=1, source_target_pairs={{0,4},{1,17},{2,6},{3,19},{4,8},{5,21},{6,10},{7,23},{8,12},{9,25}... | collective-permute-start | bytes 1376264 | tf_op jit(solution)/shard_map/ppermute | solution.py:21
  112.5 16.9 %copy-start.5 = (bf16[1,8,7168]{2,1,0:T(8,128)(2,1)S(1)}, bf16[1,8,7168]{2,1,0:T(8,128)(2,1)}, u32[]{:S(2)}) copy-start(bf16[1,8,7168]{2,1,0:T(8,128)(2,1)} %param.6) | copy-start | bytes 344068
  112.8 15.1 %collective-permute-start.11 = (bf16[8,7168]{1,0:T(8,128)(2,1)S(1)}, bf16[8,7168]{1,0:T(8,128)(2,1)S(1)}, u32[]{:S(2)}, u32[]{:S(2)}) collective-permute-start(bf16[8,7168]{1,0:T(8,128)(2,1)S(1)} %get-tuple-element.30), channel_id=1, source_target_pairs={{0,48},{1,13},{2,50},{3,15},{4,52},{5,1},{6,54},{7,3},{8,56},{9,5}... | collective-permute-start | bytes 344072 | tf_op jit(solution)/shard_map/ppermute | solution.py:21
  114.8 13.2 %collective-permute-start.12 = (bf16[8,7168]{1,0:T(8,128)(2,1)S(1)}, bf16[8,7168]{1,0:T(8,128)(2,1)S(1)}, u32[]{:S(2)}, u32[]{:S(2)}) collective-permute-start(bf16[8,7168]{1,0:T(8,128)(2,1)S(1)} %get-tuple-element.32), channel_id=1, source_target_pairs={{0,32},{1,9},{2,34},{3,11},{4,36},{5,13},{6,38},{7,15},{8,40},{9,1... | collective-permute-start | bytes 344072 | tf_op jit(solution)/shard_map/ppermute | solution.py:21
  123.5 6.0 %collective-permute-start.13 = (bf16[8,7168]{1,0:T(8,128)(2,1)S(1)}, bf16[8,7168]{1,0:T(8,128)(2,1)S(1)}, u32[]{:S(2)}, u32[]{:S(2)}) collective-permute-start(bf16[8,7168]{1,0:T(8,128)(2,1)S(1)} %get-tuple-element.31), channel_id=1, source_target_pairs={{0,16},{1,5},{2,18},{3,7},{4,20},{5,9},{6,22},{7,11},{8,24},{9,13}... | collective-permute-start | bytes 344072 | tf_op jit(solution)/shard_map/ppermute | solution.py:21
  124.4 7.2 %collective-permute-start.27 = (bf16[8,7168]{1,0:T(8,128)(2,1)S(1)}, bf16[8,7168]{1,0:T(8,128)(2,1)S(1)}, u32[]{:S(2)}, u32[]{:S(2)}) collective-permute-start(bf16[8,7168]{1,0:T(8,128)(2,1)S(1)} %get-tuple-element.27), channel_id=1, source_target_pairs={{0,48},{1,13},{2,50},{3,15},{4,52},{5,1},{6,54},{7,3},{8,56},{9,5}... | collective-permute-start | bytes 344072 | tf_op jit(solution)/shard_map/ppermute | solution.py:21
  127.0 6.4 %collective-permute-start.28 = (bf16[8,7168]{1,0:T(8,128)(2,1)S(1)}, bf16[8,7168]{1,0:T(8,128)(2,1)S(1)}, u32[]{:S(2)}, u32[]{:S(2)}) collective-permute-start(bf16[8,7168]{1,0:T(8,128)(2,1)S(1)} %get-tuple-element.29), channel_id=1, source_target_pairs={{0,32},{1,9},{2,34},{3,11},{4,36},{5,13},{6,38},{7,15},{8,40},{9,1... | collective-permute-start | bytes 344072 | tf_op jit(solution)/shard_map/ppermute | solution.py:21
  127.8 6.7 %collective-permute-start.29 = (bf16[8,7168]{1,0:T(8,128)(2,1)S(1)}, bf16[8,7168]{1,0:T(8,128)(2,1)S(1)}, u32[]{:S(2)}, u32[]{:S(2)}) collective-permute-start(bf16[8,7168]{1,0:T(8,128)(2,1)S(1)} %get-tuple-element.28), channel_id=1, source_target_pairs={{0,16},{1,5},{2,18},{3,7},{4,20},{5,9},{6,22},{7,11},{8,24},{9,13}... | collective-permute-start | bytes 344072 | tf_op jit(solution)/shard_map/ppermute | solution.py:21
  129.5 17.7 %collective-permute-start.14 = (f32[8,7168]{1,0:T(8,128)S(1)}, f32[8,7168]{1,0:T(8,128)S(1)}, u32[]{:S(2)}, u32[]{:S(2)}) collective-permute-start(f32[8,7168]{1,0:T(8,128)S(1)} %fusion.29), channel_id=1, source_target_pairs={{0,64},{1,65},{2,66},{3,67},{4,68},{5,69},{6,70},{7,71},{8,72},{9,... | collective-permute-start | bytes 688136 | tf_op jit(solution)/shard_map/ppermute | solution.py:121
  134.6 12.6 %collective-permute-start.30 = (bf16[8,7168]{1,0:T(8,128)(2,1)S(1)}, bf16[8,7168]{1,0:T(8,128)(2,1)S(1)}, u32[]{:S(2)}, u32[]{:S(2)}) collective-permute-start(bf16[8,7168]{1,0:T(8,128)(2,1)S(1)} %fusion.25), channel_id=1, source_target_pairs={{0,66},{1,67},{2,64},{3,65},{4,70},{5,71},{6,68},{7,69},{8,74},{9,... | collective-permute-start | bytes 344072 | tf_op jit(solution)/shard_map/ppermute | solution.py:122
where the time goes:
time: 148 us
  starting transfers between devices  50 us (34%)
  waiting for transfers between devices  47.2 us (32%)
  matrix products  28.9 us (20%)
  other arithmetic  13.4 us (9%)
  local copies, waits for them, and re-layouts  8.2 us (6%)
    ppermute x29, starting transfers between devices, moved(): return lax.ppermute(value, 'expert', pairs)  43.1 us
    ppermute x29, waiting for transfers between devices, moved(): return lax.ppermute(value, 'expert', pairs)  39.3 us
    dot_general x2, matrix products, expert_rows(): part = jnp.dot(hidden, down_mat, preferred_element_type=jnp.float32)  20.2 us
    dot_general x2, matrix products, expert_rows(): upper_act = jnp.dot(rows, upper_mat, preferred_element_type=jnp.float32)  8.73 us
    ppermute x1, waiting for transfers between devices, layer(): got_theirs = lax.ppermute(theirs, ('segment', 'expert'), cross)  7.88 us
    ppermute x1, starting transfers between devices, layer(): got_theirs = lax.ppermute(theirs, ('segment', 'expert'), cross)  4.72 us
    unnamed x14, local copies, waits for them, and re-layouts  4.55 us
    another operation x4, other arithmetic, served(): jnp.stack([first] + [moved(first, along(1, k)) for k in range(1, ring)])  3.93 us
  transfers between devices with their start and end apart: 31, of which 17 were waited for; matrix products, arithmetic and copies ran while one was open for 20% of the time, Pallas kernels for 0%

commit v1 on v0

--- a/solution.py
+++ b/solution.py
@@ -84,11 +84,13 @@
     full = width + code.shape[1]
     ring = X_SIZE
 
-    def served(block):
+    def served(block, after=None):
         first = jnp.stack([block] + [moved(block, along(0, k)) for k in range(1, ring)])
         second = jnp.stack([first] + [moved(first, along(1, k)) for k in range(1, ring)])
         other = moved(second, across_core)
         rows = jnp.stack([other, second]).reshape(-1, full)
+        if after is not None:
+            rows, _ = lax.optimization_barrier((rows, after))
         weight = decoded(rows[:, width:], groups)[:, expert]
         part = expert_rows(rows, weight, *mats).astype(jnp.bfloat16)
         half = part.shape[0] // 2
@@ -103,10 +105,10 @@
         sent = total.astype(jnp.bfloat16)
         for k in range(1, ring):
             result = result + moved(sent[k], along(0, -k)).astype(jnp.float32)
-        return result
+        return result, part
 
-    own_sum = served(col)
-    partner_sum = served(moved(col, across_z))
+    own_sum, first_part = served(col)
+    partner_sum, _ = served(moved(col, across_z), first_part)
 
     mine = tokens.astype(jnp.float32) + own_sum
     theirs = partner_sum.astype(jnp.bfloat16)

time: 148 us -> 157 us (1.061)
  the two profiles are of different devices: /device:TPU:32 before, /device:TPU:65 now
where the time goes in v1:
time: 157 us
  waiting for transfers between devices  53.9 us (34%)
  starting transfers between devices  44.5 us (28%)
  matrix products  28.8 us (18%)
  other arithmetic  17.3 us (11%)
  local copies, waits for them, and re-layouts  12.3 us (8%)
    ppermute x29, waiting for transfers between devices, moved(): return lax.ppermute(value, 'expert', pairs)  44.4 us
    ppermute x29, starting transfers between devices, moved(): return lax.ppermute(value, 'expert', pairs)  37.3 us
    dot_general x2, matrix products, expert_rows(): part = jnp.dot(hidden, down_mat, preferred_element_type=jnp.float32)  20.2 us
    ppermute x1, waiting for transfers between devices, layer(): got_theirs = lax.ppermute(theirs, ('segment', 'expert'), cross)  9.49 us
    optimization_barrier x1, local copies, waits for them, and re-layouts, served(): rows, _ = lax.optimization_barrier((rows, after))  6 us
    another operation x2, other arithmetic, served(): rows = jnp.stack([other, second]).reshape(-1, full)  5.6 us
    ppermute x1, starting transfers between devices, layer(): got_theirs = lax.ppermute(theirs, ('segment', 'expert'), cross)  5.23 us
    another operation x4, other arithmetic, served(): jnp.stack([first] + [moved(first, along(1, k)) for k in range(1, ring)])  5.1 us
  transfers between devices with their start and end apart: 31, of which 14 were waited for; matrix products, arithmetic and copies ran while one was open for 34% of the time, Pallas kernels for 0%

profile of v1, /device:TPU:65, one launch (start us, length us, event | category | flops | bytes accessed | tf_op | source)
XLA Modules:
  0.0 157.0 jit_solution(63867364370903628)
XLA Ops:
  0.0 0.8 select_reduce_fusion
  0.9 0.9 fusion.68
  1.8 2.8 %collective-permute-start.2 = (bf16[8,7296]{1,0:T(8,128)(2,1)S(1)}, bf16[8,7296]{1,0:T(8,128)(2,1)S(1)}, u32[]{:S(2)}, u32[]{:S(2)}) collective-permute-start(bf16[8,7296]{1,0:T(8,128)(2,1)S(1)} %get-tuple-element.39), channel_id=1, source_target_pairs={{0,48},{1,13},{2,50},{3,15},{4,52},{5,1},{6,54},{7,3},{8,56},{9,5}... | collective-permute-start | bytes 350216 | tf_op jit(solution)/shard_map/ppermute | solution.py:21
  5.0 0.7 collective-permute-start
  5.7 2.0 %collective-permute-done.2 = bf16[8,7296]{1,0:T(8,128)(2,1)S(1)} collective-permute-done((bf16[8,7296]{1,0:T(8,128)(2,1)S(1)}, bf16[8,7296]{1,0:T(8,128)(2,1)S(1)}, u32[]{:S(2)}, u32[]{:S(2)}) %collective-permute-start.2) | collective-permute-done | bytes 116768 | tf_op jit(solution)/shard_map/ppermute | solution.py:21
  7.6 2.5 %collective-permute-done.1 = bf16[8,7296]{1,0:T(8,128)(2,1)S(1)} collective-permute-done((bf16[8,7296]{1,0:T(8,128)(2,1)S(1)}, bf16[8,7296]{1,0:T(8,128)(2,1)S(1)}, u32[]{:S(2)}, u32[]{:S(2)}) %collective-permute-start.1) | collective-permute-done | bytes 116768 | tf_op jit(solution)/shard_map/ppermute | solution.py:21
  10.1 1.3 collective-permute-done
  11.4 2.3 %collective-permute-start.5 = (bf16[4,8,7296]{2,1,0:T(8,128)(2,1)S(1)}, bf16[4,8,7296]{2,1,0:T(8,128)(2,1)S(1)}, u32[]{:S(2)}, u32[]{:S(2)}) collective-permute-start(bf16[4,8,7296]{2,1,0:T(8,128)(2,1)S(1)} %get-tuple-element.28), channel_id=1, source_target_pairs={{0,12},{1,49},{2,14},{3,51},{4,0},{5,53},{6,2},{7,55},{8,4},{9,57}... | collective-permute-start | bytes 1400840 | tf_op jit(solution)/shard_map/ppermute | solution.py:21
  14.2 0.6 collective-permute-start.3
  14.8 5.1 %collective-permute-start.15 = (bf16[8,7296]{1,0:T(8,128)(2,1)S(1)}, bf16[8,7296]{1,0:T(8,128)(2,1)S(1)}, u32[]{:S(2)}, u32[]{:S(2)}) collective-permute-start(bf16[8,7296]{1,0:T(8,128)(2,1)S(1)} %get-tuple-element.39), channel_id=1, source_target_pairs={{0,2},{1,3},{2,0},{3,1},{4,6},{5,7},{6,4},{7,5},{8,10},{9,11},{10,... | collective-permute-start | bytes 350216 | tf_op jit(solution)/shard_map/ppermute | solution.py:21
  19.9 3.9 %collective-permute-done.15 = bf16[8,7296]{1,0:T(8,128)(2,1)S(1)} collective-permute-done((bf16[8,7296]{1,0:T(8,128)(2,1)S(1)}, bf16[8,7296]{1,0:T(8,128)(2,1)S(1)}, u32[]{:S(2)}, u32[]{:S(2)}) %collective-permute-start.15) | collective-permute-done | bytes 116768 | tf_op jit(solution)/shard_map/ppermute | solution.py:21
  25.3 2.6 %collective-permute-done.3 = bf16[4,8,7296]{2,1,0:T(8,128)(2,1)S(1)} collective-permute-done((bf16[4,8,7296]{2,1,0:T(8,128)(2,1)S(1)}, bf16[4,8,7296]{2,1,0:T(8,128)(2,1)S(1)}, u32[]{:S(2)}, u32[]{:S(2)}) %collective-permute-start.3) | collective-permute-done | bytes 466976 | tf_op jit(solution)/shard_map/ppermute | solution.py:21
  27.9 1.6 %pad_maximum_fusion.2 = (bf16[4,4,8,7296]{3,2,1,0:T(8,128)(2,1)}, bf16[1,4,4,8,7296]{4,3,2,1,0:T(8,128)(2,1)S(1)}) fusion(bf16[1,4,8,7296]{3,2,1,0:T(8,128)(2,1)S(1)} %bitcast.115, bf16[1,4,8,7296]{3,2,1,0:T(8,128)(2,1)S(1)} %bitcast.116, bf16[1,4,8,7296]{3,2,1,0:T(8,128)(2,1)S(1)} %bitcast.117, bf16[1,4,8,7296]{3,2,1,0:T(8,128)(2,1)S(1)} %get-tuple-element.27), kind=kLoop, calls=%fused_computation.22 | loop fusion | flops 2801664 | bytes 5603328 | tf_op jit(solution)/shard_map/stack | solution.py:89
  29.5 5.7 %collective-permute-start.6 = (bf16[4,4,8,7296]{3,2,1,0:T(8,128)(2,1)}, bf16[4,4,8,7296]{3,2,1,0:T(8,128)(2,1)}, u32[]{:S(2)}, u32[]{:S(2)}) collective-permute-start(bf16[4,4,8,7296]{3,2,1,0:T(8,128)(2,1)} %get-tuple-element.17), channel_id=1, source_target_pairs={{0,1},{1,0},{2,3},{3,2},{4,5},{5,4},{6,7},{7,6},{8,9},{9,8},{10,11... | collective-permute-start | bytes 5603336 | tf_op jit(solution)/shard_map/ppermute | solution.py:21
  36.1 0.8 collective-permute-start.19
  36.9 6.2 %collective-permute-done.21 = bf16[4,8,7296]{2,1,0:T(8,128)(2,1)S(1)} collective-permute-done((bf16[4,8,7296]{2,1,0:T(8,128)(2,1)S(1)}, bf16[4,8,7296]{2,1,0:T(8,128)(2,1)S(1)}, u32[]{:S(2)}, u32[]{:S(2)}) %collective-permute-start.21) | collective-permute-done | bytes 466976 | tf_op jit(solution)/shard_map/ppermute | solution.py:21
  43.2 1.8 %collective-permute-done.20 = bf16[4,8,7296]{2,1,0:T(8,128)(2,1)} collective-permute-done((bf16[4,8,7296]{2,1,0:T(8,128)(2,1)S(1)}, bf16[4,8,7296]{2,1,0:T(8,128)(2,1)}, u32[]{:S(2)}, u32[]{:S(2)}) %collective-permute-start.20) | collective-permute-done | bytes 466976 | tf_op jit(solution)/shard_map/ppermute | solution.py:21
  45.0 5.0 %collective-permute-done.19 = bf16[4,8,7296]{2,1,0:T(8,128)(2,1)} collective-permute-done((bf16[4,8,7296]{2,1,0:T(8,128)(2,1)S(1)}, bf16[4,8,7296]{2,1,0:T(8,128)(2,1)}, u32[]{:S(2)}, u32[]{:S(2)}) %collective-permute-start.19) | collective-permute-done | bytes 466976 | tf_op jit(solution)/shard_map/ppermute | solution.py:21
  49.9 3.3 %pad_maximum_fusion.3 = (bf16[4,4,8,7296]{3,2,1,0:T(8,128)(2,1)}, bf16[1,4,4,8,7296]{4,3,2,1,0:T(8,128)(2,1)}) fusion(bf16[1,4,8,7296]{3,2,1,0:T(8,128)(2,1)S(1)} %bitcast.114, bf16[1,4,8,7296]{3,2,1,0:T(8,128)(2,1)} %bitcast.32, bf16[1,4,8,7296]{3,2,1,0:T(8,128)(2,1)} %bitcast.31, bf16[1,4,8,7296]{3,2,1,0:T(8,128)(2,1)S(1)} %get-tuple-element.25), kind=kLoop, calls=%fused_computation.23 | loop fusion | flops 2801664 | bytes 5603328 | tf_op jit(solution)/shard_map/stack | solution.py:89
  53.3 4.5 %collective-permute-start.22 = (bf16[4,4,8,7296]{3,2,1,0:T(8,128)(2,1)}, bf16[4,4,8,7296]{3,2,1,0:T(8,128)(2,1)}, u32[]{:S(2)}, u32[]{:S(2)}) collective-permute-start(bf16[4,4,8,7296]{3,2,1,0:T(8,128)(2,1)} %get-tuple-element.15), channel_id=1, source_target_pairs={{0,1},{1,0},{2,3},{3,2},{4,5},{5,4},{6,7},{7,6},{8,9},{9,8},{10,11... | collective-permute-start | bytes 5603336 | tf_op jit(solution)/shard_map/ppermute | solution.py:21
  57.7 1.9 %pad_maximum_fusion = bf16[2,4,4,8,7296]{4,3,2,1,0:T(8,128)(2,1)S(1)} fusion(bf16[1,4,4,8,7296]{4,3,2,1,0:T(8,128)(2,1)S(1)} %get-tuple-element.18, bf16[1,4,4,8,7296]{4,3,2,1,0:T(8,128)(2,1)} %bitcast.11), kind=kLoop, calls=%fused_computation.8 | loop fusion | flops 1867776 | bytes 7471104 | tf_op jit(solution)/shard_map/stack | solution.py:91
  59.7 1.8 %copy-done.1 = bf16[2,4,4,8,7296]{4,3,2,1,0:T(8,128)(2,1)} copy-done((bf16[2,4,4,8,7296]{4,3,2,1,0:T(8,128)(2,1)}, bf16[2,4,4,8,7296]{4,3,2,1,0:T(8,128)(2,1)S(1)}, u32[]{:S(2)}) %copy-start.1) | copy-done | bytes 3735576
  61.6 4.3 %fusion.10 = f32[256,256]{1,0:T(8,128)S(1)} fusion(bf16[256,7296]{1,0:T(8,128)(2,1)} %bitcast.112, bf16[7168,256]{1,0:T(8,128)(2,1)} %bitcast.132), kind=kOutput, calls=%fused_computation.16 | convolution fusion | flops 956301312 | bytes 7667712 | tf_op jit(solution)/shard_map/dot_general | solution.py:44
  65.9 10.1 %fusion.5 = bf16[256,7168]{1,0:T(8,128)(2,1)} fusion(bf16[1,1,256,7168]{3,2,1,0:T(8,128)(2,1)} %param.11, f32[256]{0:T(256)S(1)} %bitcast.129, f32[256,256]{1,0:T(8,128)S(1)} %fusion.10, bf16[256,7296]{1,0:T(8,128)(2,1)} %bitcast.113, bf16[7168,256]{1,0:T(8,128)(2,1)} %bitcast.130), kind=kOutput, calls=%fused_computation.7 | convolution fusion | flops 1903558656 | bytes 15008768 | tf_op jit(solution)/shard_map/dot_general | solution.py:46
  76.1 1.8 %slice.125 = bf16[128,7168]{1,0:T(8,128)(2,1)S(1)} slice(bf16[256,7168]{1,0:T(8,128)(2,1)} %fusion.5), slice={[0:128], [0:7168]} | slice | bytes 3670016 | tf_op jit(solution)/shard_map/slice | solution.py:97
  78.1 3.7 %pad_maximum_fusion.1 = bf16[2,4,4,8,7296]{4,3,2,1,0:T(8,128)(2,1)} fusion(bf16[1,4,4,8,7296]{4,3,2,1,0:T(8,128)(2,1)S(1)} %copy-done, bf16[1,4,4,8,7296]{4,3,2,1,0:T(8,128)(2,1)} %bitcast.34), kind=kLoop, calls=%fused_computation.9 | loop fusion | flops 1867776 | bytes 7471104 | tf_op jit(solution)/shard_map/stack | solution.py:91
  81.8 6.0 %copy.10 = bf16[256,7296]{0,1:T(8,128)(2,1)} copy(bf16[256,7296]{1,0:T(8,128)(2,1)} %bitcast.108) | data formatting | bytes 7471104 | tf_op jit(solution)/shard_map/optimization_barrier | solution.py:93
  87.8 0.8 slice_convert_fusion
  88.7 4.3 %fusion.12 = f32[256,256]{1,0:T(8,128)S(1)} fusion(bf16[256,7296]{1,0:T(8,128)(2,1)} %bitcast.109, bf16[7168,256]{1,0:T(8,128)(2,1)} %bitcast.131), kind=kOutput, calls=%fused_computation.18 | convolution fusion | flops 956301312 | bytes 7667712 | tf_op jit(solution)/shard_map/dot_general | solution.py:43
  93.0 10.0 %fusion.2 = bf16[256,7168]{1,0:T(8,128)(2,1)} fusion(bf16[1,1,256,7168]{3,2,1,0:T(8,128)(2,1)} %param.11, f32[256]{0:T(256)S(1)} %bitcast.128, bf16[256,7296]{1,0:T(8,128)(2,1)} %bitcast.110, bf16[7168,256]{1,0:T(8,128)(2,1)} %bitcast.133, f32[256,256]{1,0:T(8,128)S(1)} %fusion.12), kind=kOutput, calls=%fused_computation.3 | convolution fusion | flops 1903558656 | bytes 15008768 | tf_op jit(solution)/shard_map/dot_general | solution.py:46
  103.1 1.8 %slice.139 = bf16[128,7168]{1,0:T(8,128)(2,1)S(1)} slice(bf16[256,7168]{1,0:T(8,128)(2,1)} %fusion.2), slice={[0:128], [0:7168]} | slice | bytes 3670016 | tf_op jit(solution)/shard_map/slice | solution.py:97
  105.6 2.2 %convert_add_fusion.1 = (f32[128,7168]{1,0:T(8,128)S(1)}, bf16[128,7168]{1,0:T(8,128)(2,1)S(1)}) fusion(bf16[128,7168]{1,0:T(8,128)(2,1)} %collective-permute-done.7, bf16[256,7168]{1,0:T(8,128)(2,1)S(1)} %copy-done.2), kind=kLoop, calls=%fused_computation.13 | loop fusion | flops 3670016 | bytes 9175040 | tf_op jit(solution)/shard_map/add | solution.py:98
  108.0 1.3 collective-permute-start.9
  109.3 1.4 collective-permute-start.8
  111.3 0.7 collective-permute-start.26
  112.0 1.9 %collective-permute-start.25 = (bf16[4,8,7168]{2,1,0:T(8,128)(2,1)S(1)}, bf16[4,8,7168]{2,1,0:T(8,128)(2,1)S(1)}, u32[]{:S(2)}, u32[]{:S(2)}) collective-permute-start(bf16[4,8,7168]{2,1,0:T(8,128)(2,1)S(1)} %get-tuple-element.21), channel_id=1, source_target_pairs={{0,8},{1,33},{2,10},{3,35},{4,12},{5,37},{6,14},{7,39},{8,0},{9,41... | collective-permute-start | bytes 1376264 | tf_op jit(solution)/shard_map/ppermute | solution.py:21
  113.9 7.9 %collective-permute-done.10 = bf16[4,8,7168]{2,1,0:T(8,128)(2,1)S(1)} collective-permute-done((bf16[4,8,7168]{2,1,0:T(8,128)(2,1)S(1)}, bf16[4,8,7168]{2,1,0:T(8,128)(2,1)S(1)}, u32[]{:S(2)}, u32[]{:S(2)}) %collective-permute-start.10) | collective-permute-done | bytes 458784 | tf_op jit(solution)/shard_map/ppermute | solution.py:21
  121.8 0.6 collective-permute-done.8
  122.7 1.8 %collective-permute-start.12 = (bf16[8,7168]{1,0:T(8,128)(2,1)S(1)}, bf16[8,7168]{1,0:T(8,128)(2,1)S(1)}, u32[]{:S(2)}, u32[]{:S(2)}) collective-permute-start(bf16[8,7168]{1,0:T(8,128)(2,1)S(1)} %get-tuple-element.34), channel_id=1, source_target_pairs={{0,32},{1,9},{2,34},{3,11},{4,36},{5,13},{6,38},{7,15},{8,40},{9,1... | collective-permute-start | bytes 344072 | tf_op jit(solution)/shard_map/ppermute | solution.py:21
  124.5 8.9 %collective-permute-done.26 = bf16[4,8,7168]{2,1,0:T(8,128)(2,1)S(1)} collective-permute-done((bf16[4,8,7168]{2,1,0:T(8,128)(2,1)S(1)}, bf16[4,8,7168]{2,1,0:T(8,128)(2,1)S(1)}, u32[]{:S(2)}, u32[]{:S(2)}) %collective-permute-start.26) | collective-permute-done | bytes 458784 | tf_op jit(solution)/shard_map/ppermute | solution.py:21
  133.4 1.1 collective-permute-start.11
  135.2 0.8 collective-permute-start.28
  136.0 1.7 %collective-permute-start.27 = (bf16[8,7168]{1,0:T(8,128)(2,1)S(1)}, bf16[8,7168]{1,0:T(8,128)(2,1)S(1)}, u32[]{:S(2)}, u32[]{:S(2)}) collective-permute-start(bf16[8,7168]{1,0:T(8,128)(2,1)S(1)} %get-tuple-element.29), channel_id=1, source_target_pairs={{0,48},{1,13},{2,50},{3,15},{4,52},{5,1},{6,54},{7,3},{8,56},{9,5}... | collective-permute-start | bytes 344072 | tf_op jit(solution)/shard_map/ppermute | solution.py:21
  137.8 2.0 %collective-permute-start.14 = (f32[8,7168]{1,0:T(8,128)S(1)}, f32[8,7168]{1,0:T(8,128)S(1)}, u32[]{:S(2)}, u32[]{:S(2)}) collective-permute-start(f32[8,7168]{1,0:T(8,128)S(1)} %fusion.42), channel_id=1, source_target_pairs={{0,64},{1,65},{2,66},{3,67},{4,68},{5,69},{6,70},{7,71},{8,72},{9,... | collective-permute-start | bytes 688136 | tf_op jit(solution)/shard_map/ppermute | solution.py:123
  139.8 1.2 collective-permute-done.29
  141.6 5.2 %collective-permute-start.30 = (bf16[8,7168]{1,0:T(8,128)(2,1)S(1)}, bf16[8,7168]{1,0:T(8,128)(2,1)S(1)}, u32[]{:S(2)}, u32[]{:S(2)}) collective-permute-start(bf16[8,7168]{1,0:T(8,128)(2,1)S(1)} %fusion.38), channel_id=1, source_target_pairs={{0,66},{1,67},{2,64},{3,65},{4,70},{5,71},{6,68},{7,69},{8,74},{9,... | collective-permute-start | bytes 344072 | tf_op jit(solution)/shard_map/ppermute | solution.py:124
  146.8 9.5 %collective-permute-done.30 = bf16[8,7168]{1,0:T(8,128)(2,1)S(1)} collective-permute-done((bf16[8,7168]{1,0:T(8,128)(2,1)S(1)}, bf16[8,7168]{1,0:T(8,128)(2,1)S(1)}, u32[]{:S(2)}, u32[]{:S(2)}) %collective-permute-start.30) | collective-permute-done | bytes 114720 | tf_op jit(solution)/shard_map/ppermute | solution.py:124
  156.3 0.7 fusion.49
  (59 shorter events, 7.2 us)
Async XLA Ops:
  1.8 5.8 %collective-permute-start.2 = (bf16[8,7296]{1,0:T(8,128)(2,1)S(1)}, bf16[8,7296]{1,0:T(8,128)(2,1)S(1)}, u32[]{:S(2)}, u32[]{:S(2)}) collective-permute-start(bf16[8,7296]{1,0:T(8,128)(2,1)S(1)} %get-tuple-element.39), channel_id=1, source_target_pairs={{0,48},{1,13},{2,50},{3,15},{4,52},{5,1},{6,54},{7,3},{8,56},{9,5}... | collective-permute-start | bytes 350216 | tf_op jit(solution)/shard_map/ppermute | solution.py:21
  4.6 5.5 %collective-permute-start.1 = (bf16[8,7296]{1,0:T(8,128)(2,1)S(1)}, bf16[8,7296]{1,0:T(8,128)(2,1)S(1)}, u32[]{:S(2)}, u32[]{:S(2)}) collective-permute-start(bf16[8,7296]{1,0:T(8,128)(2,1)S(1)} %get-tuple-element.39), channel_id=1, source_target_pairs={{0,32},{1,9},{2,34},{3,11},{4,36},{5,13},{6,38},{7,15},{8,40},{9,1... | collective-permute-start | bytes 350216 | tf_op jit(solution)/shard_map/ppermute | solution.py:21
  5.0 6.4 %collective-permute-start = (bf16[8,7296]{1,0:T(8,128)(2,1)S(1)}, bf16[8,7296]{1,0:T(8,128)(2,1)S(1)}, u32[]{:S(2)}, u32[]{:S(2)}) collective-permute-start(bf16[8,7296]{1,0:T(8,128)(2,1)S(1)} %get-tuple-element.39), channel_id=1, source_target_pairs={{0,16},{1,5},{2,18},{3,7},{4,20},{5,9},{6,22},{7,11},{8,24},{9,13}... | collective-permute-start | bytes 350216 | tf_op jit(solution)/shard_map/ppermute | solution.py:21
  11.4 13.3 %collective-permute-start.5 = (bf16[4,8,7296]{2,1,0:T(8,128)(2,1)S(1)}, bf16[4,8,7296]{2,1,0:T(8,128)(2,1)S(1)}, u32[]{:S(2)}, u32[]{:S(2)}) collective-permute-start(bf16[4,8,7296]{2,1,0:T(8,128)(2,1)S(1)} %get-tuple-element.28), channel_id=1, source_target_pairs={{0,12},{1,49},{2,14},{3,51},{4,0},{5,53},{6,2},{7,55},{8,4},{9,57}... | collective-permute-start | bytes 1400840 | tf_op jit(solution)/shard_map/ppermute | solution.py:21
  13.7 11.6 %collective-permute-start.4 = (bf16[4,8,7296]{2,1,0:T(8,128)(2,1)S(1)}, bf16[4,8,7296]{2,1,0:T(8,128)(2,1)S(1)}, u32[]{:S(2)}, u32[]{:S(2)}) collective-permute-start(bf16[4,8,7296]{2,1,0:T(8,128)(2,1)S(1)} %get-tuple-element.28), channel_id=1, source_target_pairs={{0,8},{1,33},{2,10},{3,35},{4,12},{5,37},{6,14},{7,39},{8,0},{9,41... | collective-permute-start | bytes 1400840 | tf_op jit(solution)/shard_map/ppermute | solution.py:21
  14.2 13.7 %collective-permute-start.3 = (bf16[4,8,7296]{2,1,0:T(8,128)(2,1)S(1)}, bf16[4,8,7296]{2,1,0:T(8,128)(2,1)S(1)}, u32[]{:S(2)}, u32[]{:S(2)}) collective-permute-start(bf16[4,8,7296]{2,1,0:T(8,128)(2,1)S(1)} %get-tuple-element.28), channel_id=1, source_target_pairs={{0,4},{1,17},{2,6},{3,19},{4,8},{5,21},{6,10},{7,23},{8,12},{9,25}... | collective-permute-start | bytes 1400840 | tf_op jit(solution)/shard_map/ppermute | solution.py:21
  14.8 9.0 %collective-permute-start.15 = (bf16[8,7296]{1,0:T(8,128)(2,1)S(1)}, bf16[8,7296]{1,0:T(8,128)(2,1)S(1)}, u32[]{:S(2)}, u32[]{:S(2)}) collective-permute-start(bf16[8,7296]{1,0:T(8,128)(2,1)S(1)} %get-tuple-element.39), channel_id=1, source_target_pairs={{0,2},{1,3},{2,0},{3,1},{4,6},{5,7},{6,4},{7,5},{8,10},{9,11},{10,... | collective-permute-start | bytes 350216 | tf_op jit(solution)/shard_map/ppermute | solution.py:21
  23.8 11.5 %collective-permute-start.18 = (bf16[8,7296]{1,0:T(8,128)(2,1)S(1)}, bf16[8,7296]{1,0:T(8,128)(2,1)S(1)}, u32[]{:S(2)}, u32[]{:S(2)}) collective-permute-start(bf16[8,7296]{1,0:T(8,128)(2,1)S(1)} %collective-permute-done.15), channel_id=1, source_target_pairs={{0,48},{1,13},{2,50},{3,15},{4,52},{5,1},{6,54},{7,3},{8,56},{9,5}... | collective-permute-start | bytes 350216 | tf_op jit(solution)/shard_map/ppermute | solution.py:21
  24.4 10.9 %collective-permute-start.17 = (bf16[8,7296]{1,0:T(8,128)(2,1)S(1)}, bf16[8,7296]{1,0:T(8,128)(2,1)S(1)}, u32[]{:S(2)}, u32[]{:S(2)}) collective-permute-start(bf16[8,7296]{1,0:T(8,128)(2,1)S(1)} %collective-permute-done.15), channel_id=1, source_target_pairs={{0,32},{1,9},{2,34},{3,11},{4,36},{5,13},{6,38},{7,15},{8,40},{9,1... | collective-permute-start | bytes 350216 | tf_op jit(solution)/shard_map/ppermute | solution.py:21
  24.7 10.6 %collective-permute-start.16 = (bf16[8,7296]{1,0:T(8,128)(2,1)S(1)}, bf16[8,7296]{1,0:T(8,128)(2,1)S(1)}, u32[]{:S(2)}, u32[]{:S(2)}) collective-permute-start(bf16[8,7296]{1,0:T(8,128)(2,1)S(1)} %collective-permute-done.15), channel_id=1, source_target_pairs={{0,16},{1,5},{2,18},{3,7},{4,20},{5,9},{6,22},{7,11},{8,24},{9,13}... | collective-permute-start | bytes 350216 | tf_op jit(solution)/shard_map/ppermute | solution.py:21
  29.5 28.2 %collective-permute-start.6 = (bf16[4,4,8,7296]{3,2,1,0:T(8,128)(2,1)}, bf16[4,4,8,7296]{3,2,1,0:T(8,128)(2,1)}, u32[]{:S(2)}, u32[]{:S(2)}) collective-permute-start(bf16[4,4,8,7296]{3,2,1,0:T(8,128)(2,1)} %get-tuple-element.17), channel_id=1, source_target_pairs={{0,1},{1,0},{2,3},{3,2},{4,5},{5,4},{6,7},{7,6},{8,9},{9,8},{10,11... | collective-permute-start | bytes 5603336 | tf_op jit(solution)/shard_map/ppermute | solution.py:21
  35.4 7.8 %collective-permute-start.21 = (bf16[4,8,7296]{2,1,0:T(8,128)(2,1)S(1)}, bf16[4,8,7296]{2,1,0:T(8,128)(2,1)S(1)}, u32[]{:S(2)}, u32[]{:S(2)}) collective-permute-start(bf16[4,8,7296]{2,1,0:T(8,128)(2,1)S(1)} %get-tuple-element.26), channel_id=1, source_target_pairs={{0,12},{1,49},{2,14},{3,51},{4,0},{5,53},{6,2},{7,55},{8,4},{9,57}... | collective-permute-start | bytes 1400840 | tf_op jit(solution)/shard_map/ppermute | solution.py:21
  35.6 9.4 %collective-permute-start.20 = (bf16[4,8,7296]{2,1,0:T(8,128)(2,1)S(1)}, bf16[4,8,7296]{2,1,0:T(8,128)(2,1)}, u32[]{:S(2)}, u32[]{:S(2)}) collective-permute-start(bf16[4,8,7296]{2,1,0:T(8,128)(2,1)S(1)} %get-tuple-element.26), channel_id=1, source_target_pairs={{0,8},{1,33},{2,10},{3,35},{4,12},{5,37},{6,14},{7,39},{8,0},{9,41... | collective-permute-start | bytes 1400840 | tf_op jit(solution)/shard_map/ppermute | solution.py:21
  36.1 13.9 %collective-permute-start.19 = (bf16[4,8,7296]{2,1,0:T(8,128)(2,1)S(1)}, bf16[4,8,7296]{2,1,0:T(8,128)(2,1)}, u32[]{:S(2)}, u32[]{:S(2)}) collective-permute-start(bf16[4,8,7296]{2,1,0:T(8,128)(2,1)S(1)} %get-tuple-element.26), channel_id=1, source_target_pairs={{0,4},{1,17},{2,6},{3,19},{4,8},{5,21},{6,10},{7,23},{8,12},{9,25}... | collective-permute-start | bytes 1400840 | tf_op jit(solution)/shard_map/ppermute | solution.py:21
  53.3 24.7 %collective-permute-start.22 = (bf16[4,4,8,7296]{3,2,1,0:T(8,128)(2,1)}, bf16[4,4,8,7296]{3,2,1,0:T(8,128)(2,1)}, u32[]{:S(2)}, u32[]{:S(2)}) collective-permute-start(bf16[4,4,8,7296]{3,2,1,0:T(8,128)(2,1)} %get-tuple-element.15), channel_id=1, source_target_pairs={{0,1},{1,0},{2,3},{3,2},{4,5},{5,4},{6,7},{7,6},{8,9},{9,8},{10,11... | collective-permute-start | bytes 5603336 | tf_op jit(solution)/shard_map/ppermute | solution.py:21
  59.6 1.8 %copy-start.1 = (bf16[2,4,4,8,7296]{4,3,2,1,0:T(8,128)(2,1)}, bf16[2,4,4,8,7296]{4,3,2,1,0:T(8,128)(2,1)S(1)}, u32[]{:S(2)}) copy-start(bf16[2,4,4,8,7296]{4,3,2,1,0:T(8,128)(2,1)S(1)} %pad_maximum_fusion) | copy-start | bytes 11206660
  76.1 2.1 %copy-start = (bf16[1,4,4,8,7296]{4,3,2,1,0:T(8,128)(2,1)S(1)}, bf16[1,4,4,8,7296]{4,3,2,1,0:T(8,128)(2,1)}, u32[]{:S(2)}) copy-start(bf16[1,4,4,8,7296]{4,3,2,1,0:T(8,128)(2,1)} %get-tuple-element.16) | copy-start | bytes 5603332
  77.8 27.4 %collective-permute-start.7 = (bf16[128,7168]{1,0:T(8,128)(2,1)S(1)}, bf16[128,7168]{1,0:T(8,128)(2,1)}, u32[]{:S(2)}, u32[]{:S(2)}) collective-permute-start(bf16[128,7168]{1,0:T(8,128)(2,1)S(1)} %slice.125), channel_id=1, source_target_pairs={{0,1},{1,0},{2,3},{3,2},{4,5},{5,4},{6,7},{7,6},{8,9},{9,8},{10,11... | collective-permute-start | bytes 5505032 | tf_op jit(solution)/shard_map/ppermute | solution.py:21
  103.1 2.6 %copy-start.2 = (bf16[256,7168]{1,0:T(8,128)(2,1)S(1)}, bf16[256,7168]{1,0:T(8,128)(2,1)}, u32[]{:S(2)}) copy-start(bf16[256,7168]{1,0:T(8,128)(2,1)} %fusion.5) | copy-start | bytes 11010052
  104.8 5.9 %collective-permute-start.23 = (bf16[128,7168]{1,0:T(8,128)(2,1)S(1)}, bf16[128,7168]{1,0:T(8,128)(2,1)S(1)}, u32[]{:S(2)}, u32[]{:S(2)}) collective-permute-start(bf16[128,7168]{1,0:T(8,128)(2,1)S(1)} %slice.139), channel_id=1, source_target_pairs={{0,1},{1,0},{2,3},{3,2},{4,5},{5,4},{6,7},{7,6},{8,9},{9,8},{10,11... | collective-permute-start | bytes 5505032 | tf_op jit(solution)/shard_map/ppermute | solution.py:21
  105.6 5.0 %copy-start.3 = (bf16[256,7168]{1,0:T(8,128)(2,1)S(1)}, bf16[256,7168]{1,0:T(8,128)(2,1)}, u32[]{:S(2)}) copy-start(bf16[256,7168]{1,0:T(8,128)(2,1)} %fusion.2) | copy-start | bytes 11010052
  107.9 13.8 %collective-permute-start.10 = (bf16[4,8,7168]{2,1,0:T(8,128)(2,1)S(1)}, bf16[4,8,7168]{2,1,0:T(8,128)(2,1)S(1)}, u32[]{:S(2)}, u32[]{:S(2)}) collective-permute-start(bf16[4,8,7168]{2,1,0:T(8,128)(2,1)S(1)} %get-tuple-element.23), channel_id=1, source_target_pairs={{0,4},{1,17},{2,6},{3,19},{4,8},{5,21},{6,10},{7,23},{8,12},{9,25}... | collective-permute-start | bytes 1376264 | tf_op jit(solution)/shard_map/ppermute | solution.py:21
  108.0 13.7 %collective-permute-start.9 = (bf16[4,8,7168]{2,1,0:T(8,128)(2,1)S(1)}, bf16[4,8,7168]{2,1,0:T(8,128)(2,1)S(1)}, u32[]{:S(2)}, u32[]{:S(2)}) collective-permute-start(bf16[4,8,7168]{2,1,0:T(8,128)(2,1)S(1)} %get-tuple-element.24), channel_id=1, source_target_pairs={{0,8},{1,33},{2,10},{3,35},{4,12},{5,37},{6,14},{7,39},{8,0},{9,41... | collective-permute-start | bytes 1376264 | tf_op jit(solution)/shard_map/ppermute | solution.py:21
  109.3 13.1 %collective-permute-start.8 = (bf16[4,8,7168]{2,1,0:T(8,128)(2,1)S(1)}, bf16[4,8,7168]{2,1,0:T(8,128)(2,1)S(1)}, u32[]{:S(2)}, u32[]{:S(2)}) collective-permute-start(bf16[4,8,7168]{2,1,0:T(8,128)(2,1)S(1)} %get-tuple-element.22), channel_id=1, source_target_pairs={{0,12},{1,49},{2,14},{3,51},{4,0},{5,53},{6,2},{7,55},{8,4},{9,57}... | collective-permute-start | bytes 1376264 | tf_op jit(solution)/shard_map/ppermute | solution.py:21
  111.3 22.1 %collective-permute-start.26 = (bf16[4,8,7168]{2,1,0:T(8,128)(2,1)S(1)}, bf16[4,8,7168]{2,1,0:T(8,128)(2,1)S(1)}, u32[]{:S(2)}, u32[]{:S(2)}) collective-permute-start(bf16[4,8,7168]{2,1,0:T(8,128)(2,1)S(1)} %get-tuple-element.20), channel_id=1, source_target_pairs={{0,4},{1,17},{2,6},{3,19},{4,8},{5,21},{6,10},{7,23},{8,12},{9,25}... | collective-permute-start | bytes 1376264 | tf_op jit(solution)/shard_map/ppermute | solution.py:21
  112.0 22.5 %collective-permute-start.25 = (bf16[4,8,7168]{2,1,0:T(8,128)(2,1)S(1)}, bf16[4,8,7168]{2,1,0:T(8,128)(2,1)S(1)}, u32[]{:S(2)}, u32[]{:S(2)}) collective-permute-start(bf16[4,8,7168]{2,1,0:T(8,128)(2,1)S(1)} %get-tuple-element.21), channel_id=1, source_target_pairs={{0,8},{1,33},{2,10},{3,35},{4,12},{5,37},{6,14},{7,39},{8,0},{9,41... | collective-permute-start | bytes 1376264 | tf_op jit(solution)/shard_map/ppermute | solution.py:21
  121.7 12.7 %collective-permute-start.24 = (bf16[4,8,7168]{2,1,0:T(8,128)(2,1)S(1)}, bf16[4,8,7168]{2,1,0:T(8,128)(2,1)S(1)}, u32[]{:S(2)}, u32[]{:S(2)}) collective-permute-start(bf16[4,8,7168]{2,1,0:T(8,128)(2,1)S(1)} %get-tuple-element.19), channel_id=1, source_target_pairs={{0,12},{1,49},{2,14},{3,51},{4,0},{5,53},{6,2},{7,55},{8,4},{9,57}... | collective-permute-start | bytes 1376264 | tf_op jit(solution)/shard_map/ppermute | solution.py:21
  122.4 15.3 %copy-start.4 = (bf16[1,8,7168]{2,1,0:T(8,128)(2,1)S(1)}, bf16[1,8,7168]{2,1,0:T(8,128)(2,1)}, u32[]{:S(2)}) copy-start(bf16[1,8,7168]{2,1,0:T(8,128)(2,1)} %param.6) | copy-start | bytes 344068
  122.6 13.4 %collective-permute-start.13 = (bf16[8,7168]{1,0:T(8,128)(2,1)S(1)}, bf16[8,7168]{1,0:T(8,128)(2,1)S(1)}, u32[]{:S(2)}, u32[]{:S(2)}) collective-permute-start(bf16[8,7168]{1,0:T(8,128)(2,1)S(1)} %get-tuple-element.33), channel_id=1, source_target_pairs={{0,16},{1,5},{2,18},{3,7},{4,20},{5,9},{6,22},{7,11},{8,24},{9,13}... | collective-permute-start | bytes 344072 | tf_op jit(solution)/shard_map/ppermute | solution.py:21
  122.7 15.0 %collective-permute-start.12 = (bf16[8,7168]{1,0:T(8,128)(2,1)S(1)}, bf16[8,7168]{1,0:T(8,128)(2,1)S(1)}, u32[]{:S(2)}, u32[]{:S(2)}) collective-permute-start(bf16[8,7168]{1,0:T(8,128)(2,1)S(1)} %get-tuple-element.34), channel_id=1, source_target_pairs={{0,32},{1,9},{2,34},{3,11},{4,36},{5,13},{6,38},{7,15},{8,40},{9,1... | collective-permute-start | bytes 344072 | tf_op jit(solution)/shard_map/ppermute | solution.py:21
  133.4 4.3 %collective-permute-start.11 = (bf16[8,7168]{1,0:T(8,128)(2,1)S(1)}, bf16[8,7168]{1,0:T(8,128)(2,1)S(1)}, u32[]{:S(2)}, u32[]{:S(2)}) collective-permute-start(bf16[8,7168]{1,0:T(8,128)(2,1)S(1)} %get-tuple-element.32), channel_id=1, source_target_pairs={{0,48},{1,13},{2,50},{3,15},{4,52},{5,1},{6,54},{7,3},{8,56},{9,5}... | collective-permute-start | bytes 344072 | tf_op jit(solution)/shard_map/ppermute | solution.py:21
  134.7 6.2 %collective-permute-start.29 = (bf16[8,7168]{1,0:T(8,128)(2,1)S(1)}, bf16[8,7168]{1,0:T(8,128)(2,1)S(1)}, u32[]{:S(2)}, u32[]{:S(2)}) collective-permute-start(bf16[8,7168]{1,0:T(8,128)(2,1)S(1)} %get-tuple-element.30), channel_id=1, source_target_pairs={{0,16},{1,5},{2,18},{3,7},{4,20},{5,9},{6,22},{7,11},{8,24},{9,13}... | collective-permute-start | bytes 344072 | tf_op jit(solution)/shard_map/ppermute | solution.py:21
  135.2 5.7 %collective-permute-start.28 = (bf16[8,7168]{1,0:T(8,128)(2,1)S(1)}, bf16[8,7168]{1,0:T(8,128)(2,1)S(1)}, u32[]{:S(2)}, u32[]{:S(2)}) collective-permute-start(bf16[8,7168]{1,0:T(8,128)(2,1)S(1)} %get-tuple-element.31), channel_id=1, source_target_pairs={{0,32},{1,9},{2,34},{3,11},{4,36},{5,13},{6,38},{7,15},{8,40},{9,1... | collective-permute-start | bytes 344072 | tf_op jit(solution)/shard_map/ppermute | solution.py:21
  136.0 5.5 %collective-permute-start.27 = (bf16[8,7168]{1,0:T(8,128)(2,1)S(1)}, bf16[8,7168]{1,0:T(8,128)(2,1)S(1)}, u32[]{:S(2)}, u32[]{:S(2)}) collective-permute-start(bf16[8,7168]{1,0:T(8,128)(2,1)S(1)} %get-tuple-element.29), channel_id=1, source_target_pairs={{0,48},{1,13},{2,50},{3,15},{4,52},{5,1},{6,54},{7,3},{8,56},{9,5}... | collective-permute-start | bytes 344072 | tf_op jit(solution)/shard_map/ppermute | solution.py:21
  137.8 9.0 %collective-permute-start.14 = (f32[8,7168]{1,0:T(8,128)S(1)}, f32[8,7168]{1,0:T(8,128)S(1)}, u32[]{:S(2)}, u32[]{:S(2)}) collective-permute-start(f32[8,7168]{1,0:T(8,128)S(1)} %fusion.42), channel_id=1, source_target_pairs={{0,64},{1,65},{2,66},{3,67},{4,68},{5,69},{6,70},{7,71},{8,72},{9,... | collective-permute-start | bytes 688136 | tf_op jit(solution)/shard_map/ppermute | solution.py:123
  141.6 14.7 %collective-permute-start.30 = (bf16[8,7168]{1,0:T(8,128)(2,1)S(1)}, bf16[8,7168]{1,0:T(8,128)(2,1)S(1)}, u32[]{:S(2)}, u32[]{:S(2)}) collective-permute-start(bf16[8,7168]{1,0:T(8,128)(2,1)S(1)} %fusion.38), channel_id=1, source_target_pairs={{0,66},{1,67},{2,64},{3,65},{4,70},{5,71},{6,68},{7,69},{8,74},{9,... | collective-permute-start | bytes 344072 | tf_op jit(solution)/shard_map/ppermute | solution.py:124

commit v2 on v1

--- a/solution.py
+++ b/solution.py
@@ -89,9 +89,10 @@
         second = jnp.stack([first] + [moved(first, along(1, k)) for k in range(1, ring)])
         other = moved(second, across_core)
         rows = jnp.stack([other, second]).reshape(-1, full)
+        codes = rows[:, width:]
         if after is not None:
-            rows, _ = lax.optimization_barrier((rows, after))
-        weight = decoded(rows[:, width:], groups)[:, expert]
+            codes, _ = lax.optimization_barrier((codes, after))
+        weight = decoded(codes, groups)[:, expert]
         part = expert_rows(rows, weight, *mats).astype(jnp.bfloat16)
         half = part.shape[0] // 2
         back = moved(part[:half], across_core)
@@ -107,8 +108,9 @@
             result = result + moved(sent[k], along(0, -k)).astype(jnp.float32)
         return result, part
 
+    partner_col = moved(col, across_z)
     own_sum, first_part = served(col)
-    partner_sum, _ = served(moved(col, across_z), first_part)
+    partner_sum, _ = served(partner_col, first_part)
 
     mine = tokens.astype(jnp.float32) + own_sum
     theirs = partner_sum.astype(jnp.bfloat16)

time: 157 us -> 151 us (0.962)
  local copies, waits for them, and re-layouts: 12.3 us -> 8.22 us
  other arithmetic: 17.3 us -> 14.7 us
    optimization_barrier x1, local copies, waits for them, and re-layouts: 6 us -> 0.11 us  [served(): codes, _ = lax.optimization_barrier((codes, after))]
    dot_general x1 -> x2, matrix products: 4.31 us -> 8.61 us  [expert_rows(): upper_act = jnp.dot(rows, upper_mat, preferred_element_type=jnp.float32)]
    dot_general x1 -> x0, matrix products: 4.31 us -> none  [expert_rows(): gate_act = jnp.dot(rows, gate_mat, preferred_element_type=jnp.float32)]
    another operation x2, other arithmetic: 5.6 us -> 3.8 us  [served(): rows = jnp.stack([other, second]).reshape(-1, full)]
    unnamed x11 -> x13, local copies, waits for them, and re-layouts: 2.53 us -> 4.32 us
  transfers between devices with their start and end apart: 31 -> 31, of which waited for: 14 -> 14; matrix products, arithmetic and copies ran while one was open for 34% -> 30% of each run, Pallas kernels for 0% -> 0%
where the time goes in v2:
time: 151 us; the launch traced here: 150 us
  waiting for transfers between devices  54.2 us (36%)
  starting transfers between devices  44.2 us (29%)
  matrix products  28.8 us (19%)
  other arithmetic  14.7 us (10%)
  local copies, waits for them, and re-layouts  8.22 us (5%)
    ppermute x29, waiting for transfers between devices, moved(): return lax.ppermute(value, 'expert', pairs)  44.7 us
    ppermute x29, starting transfers between devices, moved(): return lax.ppermute(value, 'expert', pairs)  37.3 us
    dot_general x2, matrix products, expert_rows(): part = jnp.dot(hidden, down_mat, preferred_element_type=jnp.float32)  20.2 us
    ppermute x1, waiting for transfers between devices, layer(): got_theirs = lax.ppermute(theirs, ('segment', 'expert'), cross)  9.49 us
    dot_general x2, matrix products, expert_rows(): upper_act = jnp.dot(rows, upper_mat, preferred_element_type=jnp.float32)  8.61 us
    another operation x4, other arithmetic, served(): jnp.stack([first] + [moved(first, along(1, k)) for k in range(1, ring)])  5.16 us
    ppermute x1, starting transfers between devices, layer(): got_theirs = lax.ppermute(theirs, ('segment', 'expert'), cross)  4.93 us
    unnamed x13, local copies, waits for them, and re-layouts  4.32 us
  transfers between devices with their start and end apart: 31, of which 14 were waited for; matrix products, arithmetic and copies ran while one was open for 30% of the time, Pallas kernels for 0%

profile of v2, /device:TPU:65, one launch (start us, length us, event | category | flops | bytes accessed | tf_op | source)
XLA Modules:
  0.0 150.3 jit_solution(11935859348566346197)
XLA Ops:
  0.0 0.8 select_reduce_fusion
  0.9 0.9 fusion.59
  1.8 2.8 %collective-permute-start.2 = (bf16[8,7296]{1,0:T(8,128)(2,1)S(1)}, bf16[8,7296]{1,0:T(8,128)(2,1)S(1)}, u32[]{:S(2)}, u32[]{:S(2)}) collective-permute-start(bf16[8,7296]{1,0:T(8,128)(2,1)S(1)} %get-tuple-element.36), channel_id=1, source_target_pairs={{0,48},{1,13},{2,50},{3,15},{4,52},{5,1},{6,54},{7,3},{8,56},{9,5}... | collective-permute-start | bytes 350216 | tf_op jit(solution)/shard_map/ppermute | solution.py:21
  5.0 0.7 collective-permute-start
  5.7 2.0 %collective-permute-done.2 = bf16[8,7296]{1,0:T(8,128)(2,1)S(1)} collective-permute-done((bf16[8,7296]{1,0:T(8,128)(2,1)S(1)}, bf16[8,7296]{1,0:T(8,128)(2,1)S(1)}, u32[]{:S(2)}, u32[]{:S(2)}) %collective-permute-start.2) | collective-permute-done | bytes 116768 | tf_op jit(solution)/shard_map/ppermute | solution.py:21
  7.6 2.5 %collective-permute-done.1 = bf16[8,7296]{1,0:T(8,128)(2,1)S(1)} collective-permute-done((bf16[8,7296]{1,0:T(8,128)(2,1)S(1)}, bf16[8,7296]{1,0:T(8,128)(2,1)S(1)}, u32[]{:S(2)}, u32[]{:S(2)}) %collective-permute-start.1) | collective-permute-done | bytes 116768 | tf_op jit(solution)/shard_map/ppermute | solution.py:21
  10.1 1.3 collective-permute-done
  11.4 2.3 %collective-permute-start.5 = (bf16[4,8,7296]{2,1,0:T(8,128)(2,1)S(1)}, bf16[4,8,7296]{2,1,0:T(8,128)(2,1)S(1)}, u32[]{:S(2)}, u32[]{:S(2)}) collective-permute-start(bf16[4,8,7296]{2,1,0:T(8,128)(2,1)S(1)} %get-tuple-element.28), channel_id=1, source_target_pairs={{0,12},{1,49},{2,14},{3,51},{4,0},{5,53},{6,2},{7,55},{8,4},{9,57}... | collective-permute-start | bytes 1400840 | tf_op jit(solution)/shard_map/ppermute | solution.py:21
  14.2 0.6 collective-permute-start.3
  14.8 5.1 %collective-permute-start.15 = (bf16[8,7296]{1,0:T(8,128)(2,1)S(1)}, bf16[8,7296]{1,0:T(8,128)(2,1)S(1)}, u32[]{:S(2)}, u32[]{:S(2)}) collective-permute-start(bf16[8,7296]{1,0:T(8,128)(2,1)S(1)} %get-tuple-element.36), channel_id=1, source_target_pairs={{0,2},{1,3},{2,0},{3,1},{4,6},{5,7},{6,4},{7,5},{8,10},{9,11},{10,... | collective-permute-start | bytes 350216 | tf_op jit(solution)/shard_map/ppermute | solution.py:21
  19.9 3.9 %collective-permute-done.15 = bf16[8,7296]{1,0:T(8,128)(2,1)S(1)} collective-permute-done((bf16[8,7296]{1,0:T(8,128)(2,1)S(1)}, bf16[8,7296]{1,0:T(8,128)(2,1)S(1)}, u32[]{:S(2)}, u32[]{:S(2)}) %collective-permute-start.15) | collective-permute-done | bytes 116768 | tf_op jit(solution)/shard_map/ppermute | solution.py:21
  25.3 2.6 %collective-permute-done.3 = bf16[4,8,7296]{2,1,0:T(8,128)(2,1)S(1)} collective-permute-done((bf16[4,8,7296]{2,1,0:T(8,128)(2,1)S(1)}, bf16[4,8,7296]{2,1,0:T(8,128)(2,1)S(1)}, u32[]{:S(2)}, u32[]{:S(2)}) %collective-permute-start.3) | collective-permute-done | bytes 466976 | tf_op jit(solution)/shard_map/ppermute | solution.py:21
  27.9 1.6 %pad_maximum_fusion.2 = (bf16[4,4,8,7296]{3,2,1,0:T(8,128)(2,1)}, bf16[1,4,4,8,7296]{4,3,2,1,0:T(8,128)(2,1)S(1)}) fusion(bf16[1,4,8,7296]{3,2,1,0:T(8,128)(2,1)S(1)} %bitcast.115, bf16[1,4,8,7296]{3,2,1,0:T(8,128)(2,1)S(1)} %bitcast.116, bf16[1,4,8,7296]{3,2,1,0:T(8,128)(2,1)S(1)} %bitcast.117, bf16[1,4,8,7296]{3,2,1,0:T(8,128)(2,1)S(1)} %get-tuple-element.27), kind=kLoop, calls=%fused_computation.22 | loop fusion | flops 2801664 | bytes 5603328 | tf_op jit(solution)/shard_map/stack | solution.py:89
  29.5 5.7 %collective-permute-start.6 = (bf16[4,4,8,7296]{3,2,1,0:T(8,128)(2,1)}, bf16[4,4,8,7296]{3,2,1,0:T(8,128)(2,1)}, u32[]{:S(2)}, u32[]{:S(2)}) collective-permute-start(bf16[4,4,8,7296]{3,2,1,0:T(8,128)(2,1)} %get-tuple-element.17), channel_id=1, source_target_pairs={{0,1},{1,0},{2,3},{3,2},{4,5},{5,4},{6,7},{7,6},{8,9},{9,8},{10,11... | collective-permute-start | bytes 5603336 | tf_op jit(solution)/shard_map/ppermute | solution.py:21
  36.1 0.8 collective-permute-start.19
  36.9 6.2 %collective-permute-done.21 = bf16[4,8,7296]{2,1,0:T(8,128)(2,1)S(1)} collective-permute-done((bf16[4,8,7296]{2,1,0:T(8,128)(2,1)S(1)}, bf16[4,8,7296]{2,1,0:T(8,128)(2,1)S(1)}, u32[]{:S(2)}, u32[]{:S(2)}) %collective-permute-start.21) | collective-permute-done | bytes 466976 | tf_op jit(solution)/shard_map/ppermute | solution.py:21
  43.1 1.8 %collective-permute-done.20 = bf16[4,8,7296]{2,1,0:T(8,128)(2,1)} collective-permute-done((bf16[4,8,7296]{2,1,0:T(8,128)(2,1)S(1)}, bf16[4,8,7296]{2,1,0:T(8,128)(2,1)}, u32[]{:S(2)}, u32[]{:S(2)}) %collective-permute-start.20) | collective-permute-done | bytes 466976 | tf_op jit(solution)/shard_map/ppermute | solution.py:21
  45.0 5.0 %collective-permute-done.19 = bf16[4,8,7296]{2,1,0:T(8,128)(2,1)} collective-permute-done((bf16[4,8,7296]{2,1,0:T(8,128)(2,1)S(1)}, bf16[4,8,7296]{2,1,0:T(8,128)(2,1)}, u32[]{:S(2)}, u32[]{:S(2)}) %collective-permute-start.19) | collective-permute-done | bytes 466976 | tf_op jit(solution)/shard_map/ppermute | solution.py:21
  49.9 3.4 %pad_maximum_fusion.3 = (bf16[4,4,8,7296]{3,2,1,0:T(8,128)(2,1)}, bf16[1,4,4,8,7296]{4,3,2,1,0:T(8,128)(2,1)}) fusion(bf16[1,4,8,7296]{3,2,1,0:T(8,128)(2,1)S(1)} %bitcast.114, bf16[1,4,8,7296]{3,2,1,0:T(8,128)(2,1)} %bitcast.32, bf16[1,4,8,7296]{3,2,1,0:T(8,128)(2,1)} %bitcast.31, bf16[1,4,8,7296]{3,2,1,0:T(8,128)(2,1)S(1)} %get-tuple-element.25), kind=kLoop, calls=%fused_computation.23 | loop fusion | flops 2801664 | bytes 5603328 | tf_op jit(solution)/shard_map/stack | solution.py:89
  53.3 4.5 %collective-permute-start.22 = (bf16[4,4,8,7296]{3,2,1,0:T(8,128)(2,1)}, bf16[4,4,8,7296]{3,2,1,0:T(8,128)(2,1)}, u32[]{:S(2)}, u32[]{:S(2)}) collective-permute-start(bf16[4,4,8,7296]{3,2,1,0:T(8,128)(2,1)} %get-tuple-element.15), channel_id=1, source_target_pairs={{0,1},{1,0},{2,3},{3,2},{4,5},{5,4},{6,7},{7,6},{8,9},{9,8},{10,11... | collective-permute-start | bytes 5603336 | tf_op jit(solution)/shard_map/ppermute | solution.py:21
  57.8 1.9 %pad_maximum_fusion = bf16[2,4,4,8,7296]{4,3,2,1,0:T(8,128)(2,1)S(1)} fusion(bf16[1,4,4,8,7296]{4,3,2,1,0:T(8,128)(2,1)S(1)} %get-tuple-element.18, bf16[1,4,4,8,7296]{4,3,2,1,0:T(8,128)(2,1)} %bitcast.11), kind=kLoop, calls=%fused_computation.8 | loop fusion | flops 1867776 | bytes 7471104 | tf_op jit(solution)/shard_map/stack | solution.py:91
  59.7 1.8 %copy-done.2 = bf16[2,4,4,8,7296]{4,3,2,1,0:T(8,128)(2,1)} copy-done((bf16[2,4,4,8,7296]{4,3,2,1,0:T(8,128)(2,1)}, bf16[2,4,4,8,7296]{4,3,2,1,0:T(8,128)(2,1)S(1)}, u32[]{:S(2)}) %copy-start.2) | copy-done | bytes 3735576
  61.7 4.3 %fusion.10 = f32[256,256]{1,0:T(8,128)S(1)} fusion(bf16[256,7296]{1,0:T(8,128)(2,1)} %bitcast.112, bf16[7168,256]{1,0:T(8,128)(2,1)} %bitcast.130), kind=kOutput, calls=%fused_computation.16 | convolution fusion | flops 956301312 | bytes 7667712 | tf_op jit(solution)/shard_map/dot_general | solution.py:44
  66.0 10.0 %fusion.5 = bf16[256,7168]{1,0:T(8,128)(2,1)} fusion(bf16[1,1,256,7168]{3,2,1,0:T(8,128)(2,1)} %param.11, f32[256]{0:T(256)S(1)} %bitcast.129, f32[256,256]{1,0:T(8,128)S(1)} %fusion.10, bf16[256,7296]{1,0:T(8,128)(2,1)} %bitcast.113, bf16[7168,256]{1,0:T(8,128)(2,1)} %bitcast.132), kind=kOutput, calls=%fused_computation.7 | convolution fusion | flops 1903558656 | bytes 15008768 | tf_op jit(solution)/shard_map/dot_general | solution.py:46
  76.1 1.8 %slice.125 = bf16[128,7168]{1,0:T(8,128)(2,1)S(1)} slice(bf16[256,7168]{1,0:T(8,128)(2,1)} %fusion.5), slice={[0:128], [0:7168]} | slice | bytes 3670016 | tf_op jit(solution)/shard_map/slice | solution.py:98
  78.1 1.9 %pad_maximum_fusion.1 = bf16[2,4,4,8,7296]{4,3,2,1,0:T(8,128)(2,1)S(1)} fusion(bf16[1,4,4,8,7296]{4,3,2,1,0:T(8,128)(2,1)S(1)} %copy-done, bf16[1,4,4,8,7296]{4,3,2,1,0:T(8,128)(2,1)} %bitcast.34), kind=kLoop, calls=%fused_computation.9 | loop fusion | flops 1867776 | bytes 7471104 | tf_op jit(solution)/shard_map/stack | solution.py:91
  80.0 1.8 %copy-done.1 = bf16[2,4,4,8,7296]{4,3,2,1,0:T(8,128)(2,1)} copy-done((bf16[2,4,4,8,7296]{4,3,2,1,0:T(8,128)(2,1)}, bf16[2,4,4,8,7296]{4,3,2,1,0:T(8,128)(2,1)S(1)}, u32[]{:S(2)}) %copy-start.1) | copy-done | bytes 3735576
  82.0 4.3 %fusion.8 = f32[256,256]{1,0:T(8,128)S(1)} fusion(bf16[256,7296]{1,0:T(8,128)(2,1)} %bitcast.109, bf16[7168,256]{1,0:T(8,128)(2,1)} %bitcast.131), kind=kOutput, calls=%fused_computation.14 | convolution fusion | flops 956301312 | bytes 7667712 | tf_op jit(solution)/shard_map/dot_general | solution.py:44
  86.3 10.1 %fusion.2 = bf16[256,7168]{1,0:T(8,128)(2,1)} fusion(bf16[1,1,256,7168]{3,2,1,0:T(8,128)(2,1)} %param.11, f32[256]{0:T(256)S(1)} %bitcast.128, f32[256,256]{1,0:T(8,128)S(1)} %fusion.8, bf16[256,7296]{1,0:T(8,128)(2,1)} %bitcast.110, bf16[7168,256]{1,0:T(8,128)(2,1)} %bitcast.133), kind=kOutput, calls=%fused_computation.3 | convolution fusion | flops 1903558656 | bytes 15008768 | tf_op jit(solution)/shard_map/dot_general | solution.py:46
  96.4 1.8 %slice.139 = bf16[128,7168]{1,0:T(8,128)(2,1)S(1)} slice(bf16[256,7168]{1,0:T(8,128)(2,1)} %fusion.2), slice={[0:128], [0:7168]} | slice | bytes 3670016 | tf_op jit(solution)/shard_map/slice | solution.py:98
  99.0 2.2 %convert_add_fusion.1 = (f32[128,7168]{1,0:T(8,128)S(1)}, bf16[128,7168]{1,0:T(8,128)(2,1)S(1)}) fusion(bf16[128,7168]{1,0:T(8,128)(2,1)} %collective-permute-done.7, bf16[256,7168]{1,0:T(8,128)(2,1)S(1)} %copy-done.3), kind=kLoop, calls=%fused_computation.13 | loop fusion | flops 3670016 | bytes 9175040 | tf_op jit(solution)/shard_map/add | solution.py:99
  101.4 1.3 collective-permute-start.9
  102.7 1.4 collective-permute-start.8
  104.7 0.7 collective-permute-start.26
  105.4 1.9 %collective-permute-start.25 = (bf16[4,8,7168]{2,1,0:T(8,128)(2,1)S(1)}, bf16[4,8,7168]{2,1,0:T(8,128)(2,1)S(1)}, u32[]{:S(2)}, u32[]{:S(2)}) collective-permute-start(bf16[4,8,7168]{2,1,0:T(8,128)(2,1)S(1)} %get-tuple-element.21), channel_id=1, source_target_pairs={{0,8},{1,33},{2,10},{3,35},{4,12},{5,37},{6,14},{7,39},{8,0},{9,41... | collective-permute-start | bytes 1376264 | tf_op jit(solution)/shard_map/ppermute | solution.py:21
  107.2 7.9 %collective-permute-done.10 = bf16[4,8,7168]{2,1,0:T(8,128)(2,1)S(1)} collective-permute-done((bf16[4,8,7168]{2,1,0:T(8,128)(2,1)S(1)}, bf16[4,8,7168]{2,1,0:T(8,128)(2,1)S(1)}, u32[]{:S(2)}, u32[]{:S(2)}) %collective-permute-start.10) | collective-permute-done | bytes 458784 | tf_op jit(solution)/shard_map/ppermute | solution.py:21
  115.1 0.6 collective-permute-done.8
  116.1 1.8 %collective-permute-start.12 = (bf16[8,7168]{1,0:T(8,128)(2,1)S(1)}, bf16[8,7168]{1,0:T(8,128)(2,1)S(1)}, u32[]{:S(2)}, u32[]{:S(2)}) collective-permute-start(bf16[8,7168]{1,0:T(8,128)(2,1)S(1)} %get-tuple-element.34), channel_id=1, source_target_pairs={{0,32},{1,9},{2,34},{3,11},{4,36},{5,13},{6,38},{7,15},{8,40},{9,1... | collective-permute-start | bytes 344072 | tf_op jit(solution)/shard_map/ppermute | solution.py:21
  117.9 8.9 %collective-permute-done.26 = bf16[4,8,7168]{2,1,0:T(8,128)(2,1)S(1)} collective-permute-done((bf16[4,8,7168]{2,1,0:T(8,128)(2,1)S(1)}, bf16[4,8,7168]{2,1,0:T(8,128)(2,1)S(1)}, u32[]{:S(2)}, u32[]{:S(2)}) %collective-permute-start.26) | collective-permute-done | bytes 458784 | tf_op jit(solution)/shard_map/ppermute | solution.py:21
  126.8 1.1 collective-permute-start.11
  128.6 0.8 collective-permute-start.28
  129.4 1.7 %collective-permute-start.27 = (bf16[8,7168]{1,0:T(8,128)(2,1)S(1)}, bf16[8,7168]{1,0:T(8,128)(2,1)S(1)}, u32[]{:S(2)}, u32[]{:S(2)}) collective-permute-start(bf16[8,7168]{1,0:T(8,128)(2,1)S(1)} %get-tuple-element.29), channel_id=1, source_target_pairs={{0,48},{1,13},{2,50},{3,15},{4,52},{5,1},{6,54},{7,3},{8,56},{9,5}... | collective-permute-start | bytes 344072 | tf_op jit(solution)/shard_map/ppermute | solution.py:21
  131.2 2.0 %collective-permute-start.14 = (f32[8,7168]{1,0:T(8,128)S(1)}, f32[8,7168]{1,0:T(8,128)S(1)}, u32[]{:S(2)}, u32[]{:S(2)}) collective-permute-start(f32[8,7168]{1,0:T(8,128)S(1)} %fusion.29), channel_id=1, source_target_pairs={{0,64},{1,65},{2,66},{3,67},{4,68},{5,69},{6,70},{7,71},{8,72},{9,... | collective-permute-start | bytes 688136 | tf_op jit(solution)/shard_map/ppermute | solution.py:125
  133.1 1.2 collective-permute-done.29
  134.3 0.9 collective-permute-done.27
  135.3 4.9 %collective-permute-start.30 = (bf16[8,7168]{1,0:T(8,128)(2,1)S(1)}, bf16[8,7168]{1,0:T(8,128)(2,1)S(1)}, u32[]{:S(2)}, u32[]{:S(2)}) collective-permute-start(bf16[8,7168]{1,0:T(8,128)(2,1)S(1)} %fusion.25), channel_id=1, source_target_pairs={{0,66},{1,67},{2,64},{3,65},{4,70},{5,71},{6,68},{7,69},{8,74},{9,... | collective-permute-start | bytes 344072 | tf_op jit(solution)/shard_map/ppermute | solution.py:126
  140.2 9.5 %collective-permute-done.30 = bf16[8,7168]{1,0:T(8,128)(2,1)S(1)} collective-permute-done((bf16[8,7168]{1,0:T(8,128)(2,1)S(1)}, bf16[8,7168]{1,0:T(8,128)(2,1)S(1)}, u32[]{:S(2)}, u32[]{:S(2)}) %collective-permute-start.30) | collective-permute-done | bytes 114720 | tf_op jit(solution)/shard_map/ppermute | solution.py:126
  149.7 0.7 fusion.40
  (61 shorter events, 6.7 us)
Async XLA Ops:
  1.8 5.8 %collective-permute-start.2 = (bf16[8,7296]{1,0:T(8,128)(2,1)S(1)}, bf16[8,7296]{1,0:T(8,128)(2,1)S(1)}, u32[]{:S(2)}, u32[]{:S(2)}) collective-permute-start(bf16[8,7296]{1,0:T(8,128)(2,1)S(1)} %get-tuple-element.36), channel_id=1, source_target_pairs={{0,48},{1,13},{2,50},{3,15},{4,52},{5,1},{6,54},{7,3},{8,56},{9,5}... | collective-permute-start | bytes 350216 | tf_op jit(solution)/shard_map/ppermute | solution.py:21
  4.6 5.5 %collective-permute-start.1 = (bf16[8,7296]{1,0:T(8,128)(2,1)S(1)}, bf16[8,7296]{1,0:T(8,128)(2,1)S(1)}, u32[]{:S(2)}, u32[]{:S(2)}) collective-permute-start(bf16[8,7296]{1,0:T(8,128)(2,1)S(1)} %get-tuple-element.36), channel_id=1, source_target_pairs={{0,32},{1,9},{2,34},{3,11},{4,36},{5,13},{6,38},{7,15},{8,40},{9,1... | collective-permute-start | bytes 350216 | tf_op jit(solution)/shard_map/ppermute | solution.py:21
  5.0 6.4 %collective-permute-start = (bf16[8,7296]{1,0:T(8,128)(2,1)S(1)}, bf16[8,7296]{1,0:T(8,128)(2,1)S(1)}, u32[]{:S(2)}, u32[]{:S(2)}) collective-permute-start(bf16[8,7296]{1,0:T(8,128)(2,1)S(1)} %get-tuple-element.36), channel_id=1, source_target_pairs={{0,16},{1,5},{2,18},{3,7},{4,20},{5,9},{6,22},{7,11},{8,24},{9,13}... | collective-permute-start | bytes 350216 | tf_op jit(solution)/shard_map/ppermute | solution.py:21
  11.4 13.3 %collective-permute-start.5 = (bf16[4,8,7296]{2,1,0:T(8,128)(2,1)S(1)}, bf16[4,8,7296]{2,1,0:T(8,128)(2,1)S(1)}, u32[]{:S(2)}, u32[]{:S(2)}) collective-permute-start(bf16[4,8,7296]{2,1,0:T(8,128)(2,1)S(1)} %get-tuple-element.28), channel_id=1, source_target_pairs={{0,12},{1,49},{2,14},{3,51},{4,0},{5,53},{6,2},{7,55},{8,4},{9,57}... | collective-permute-start | bytes 1400840 | tf_op jit(solution)/shard_map/ppermute | solution.py:21
  13.7 11.6 %collective-permute-start.4 = (bf16[4,8,7296]{2,1,0:T(8,128)(2,1)S(1)}, bf16[4,8,7296]{2,1,0:T(8,128)(2,1)S(1)}, u32[]{:S(2)}, u32[]{:S(2)}) collective-permute-start(bf16[4,8,7296]{2,1,0:T(8,128)(2,1)S(1)} %get-tuple-element.28), channel_id=1, source_target_pairs={{0,8},{1,33},{2,10},{3,35},{4,12},{5,37},{6,14},{7,39},{8,0},{9,41... | collective-permute-start | bytes 1400840 | tf_op jit(solution)/shard_map/ppermute | solution.py:21
  14.2 13.7 %collective-permute-start.3 = (bf16[4,8,7296]{2,1,0:T(8,128)(2,1)S(1)}, bf16[4,8,7296]{2,1,0:T(8,128)(2,1)S(1)}, u32[]{:S(2)}, u32[]{:S(2)}) collective-permute-start(bf16[4,8,7296]{2,1,0:T(8,128)(2,1)S(1)} %get-tuple-element.28), channel_id=1, source_target_pairs={{0,4},{1,17},{2,6},{3,19},{4,8},{5,21},{6,10},{7,23},{8,12},{9,25}... | collective-permute-start | bytes 1400840 | tf_op jit(solution)/shard_map/ppermute | solution.py:21
  14.8 9.0 %collective-permute-start.15 = (bf16[8,7296]{1,0:T(8,128)(2,1)S(1)}, bf16[8,7296]{1,0:T(8,128)(2,1)S(1)}, u32[]{:S(2)}, u32[]{:S(2)}) collective-permute-start(bf16[8,7296]{1,0:T(8,128)(2,1)S(1)} %get-tuple-element.36), channel_id=1, source_target_pairs={{0,2},{1,3},{2,0},{3,1},{4,6},{5,7},{6,4},{7,5},{8,10},{9,11},{10,... | collective-permute-start | bytes 350216 | tf_op jit(solution)/shard_map/ppermute | solution.py:21
  23.8 11.5 %collective-permute-start.18 = (bf16[8,7296]{1,0:T(8,128)(2,1)S(1)}, bf16[8,7296]{1,0:T(8,128)(2,1)S(1)}, u32[]{:S(2)}, u32[]{:S(2)}) collective-permute-start(bf16[8,7296]{1,0:T(8,128)(2,1)S(1)} %collective-permute-done.15), channel_id=1, source_target_pairs={{0,48},{1,13},{2,50},{3,15},{4,52},{5,1},{6,54},{7,3},{8,56},{9,5}... | collective-permute-start | bytes 350216 | tf_op jit(solution)/shard_map/ppermute | solution.py:21
  24.4 10.9 %collective-permute-start.17 = (bf16[8,7296]{1,0:T(8,128)(2,1)S(1)}, bf16[8,7296]{1,0:T(8,128)(2,1)S(1)}, u32[]{:S(2)}, u32[]{:S(2)}) collective-permute-start(bf16[8,7296]{1,0:T(8,128)(2,1)S(1)} %collective-permute-done.15), channel_id=1, source_target_pairs={{0,32},{1,9},{2,34},{3,11},{4,36},{5,13},{6,38},{7,15},{8,40},{9,1... | collective-permute-start | bytes 350216 | tf_op jit(solution)/shard_map/ppermute | solution.py:21
  24.7 10.5 %collective-permute-start.16 = (bf16[8,7296]{1,0:T(8,128)(2,1)S(1)}, bf16[8,7296]{1,0:T(8,128)(2,1)S(1)}, u32[]{:S(2)}, u32[]{:S(2)}) collective-permute-start(bf16[8,7296]{1,0:T(8,128)(2,1)S(1)} %collective-permute-done.15), channel_id=1, source_target_pairs={{0,16},{1,5},{2,18},{3,7},{4,20},{5,9},{6,22},{7,11},{8,24},{9,13}... | collective-permute-start | bytes 350216 | tf_op jit(solution)/shard_map/ppermute | solution.py:21
  29.5 28.3 %collective-permute-start.6 = (bf16[4,4,8,7296]{3,2,1,0:T(8,128)(2,1)}, bf16[4,4,8,7296]{3,2,1,0:T(8,128)(2,1)}, u32[]{:S(2)}, u32[]{:S(2)}) collective-permute-start(bf16[4,4,8,7296]{3,2,1,0:T(8,128)(2,1)} %get-tuple-element.17), channel_id=1, source_target_pairs={{0,1},{1,0},{2,3},{3,2},{4,5},{5,4},{6,7},{7,6},{8,9},{9,8},{10,11... | collective-permute-start | bytes 5603336 | tf_op jit(solution)/shard_map/ppermute | solution.py:21
  35.3 7.8 %collective-permute-start.21 = (bf16[4,8,7296]{2,1,0:T(8,128)(2,1)S(1)}, bf16[4,8,7296]{2,1,0:T(8,128)(2,1)S(1)}, u32[]{:S(2)}, u32[]{:S(2)}) collective-permute-start(bf16[4,8,7296]{2,1,0:T(8,128)(2,1)S(1)} %get-tuple-element.26), channel_id=1, source_target_pairs={{0,12},{1,49},{2,14},{3,51},{4,0},{5,53},{6,2},{7,55},{8,4},{9,57}... | collective-permute-start | bytes 1400840 | tf_op jit(solution)/shard_map/ppermute | solution.py:21
  35.6 9.4 %collective-permute-start.20 = (bf16[4,8,7296]{2,1,0:T(8,128)(2,1)S(1)}, bf16[4,8,7296]{2,1,0:T(8,128)(2,1)}, u32[]{:S(2)}, u32[]{:S(2)}) collective-permute-start(bf16[4,8,7296]{2,1,0:T(8,128)(2,1)S(1)} %get-tuple-element.26), channel_id=1, source_target_pairs={{0,8},{1,33},{2,10},{3,35},{4,12},{5,37},{6,14},{7,39},{8,0},{9,41... | collective-permute-start | bytes 1400840 | tf_op jit(solution)/shard_map/ppermute | solution.py:21
  36.1 13.9 %collective-permute-start.19 = (bf16[4,8,7296]{2,1,0:T(8,128)(2,1)S(1)}, bf16[4,8,7296]{2,1,0:T(8,128)(2,1)}, u32[]{:S(2)}, u32[]{:S(2)}) collective-permute-start(bf16[4,8,7296]{2,1,0:T(8,128)(2,1)S(1)} %get-tuple-element.26), channel_id=1, source_target_pairs={{0,4},{1,17},{2,6},{3,19},{4,8},{5,21},{6,10},{7,23},{8,12},{9,25}... | collective-permute-start | bytes 1400840 | tf_op jit(solution)/shard_map/ppermute | solution.py:21
  53.3 24.6 %collective-permute-start.22 = (bf16[4,4,8,7296]{3,2,1,0:T(8,128)(2,1)}, bf16[4,4,8,7296]{3,2,1,0:T(8,128)(2,1)}, u32[]{:S(2)}, u32[]{:S(2)}) collective-permute-start(bf16[4,4,8,7296]{3,2,1,0:T(8,128)(2,1)} %get-tuple-element.15), channel_id=1, source_target_pairs={{0,1},{1,0},{2,3},{3,2},{4,5},{5,4},{6,7},{7,6},{8,9},{9,8},{10,11... | collective-permute-start | bytes 5603336 | tf_op jit(solution)/shard_map/ppermute | solution.py:21
  59.7 1.8 %copy-start.2 = (bf16[2,4,4,8,7296]{4,3,2,1,0:T(8,128)(2,1)}, bf16[2,4,4,8,7296]{4,3,2,1,0:T(8,128)(2,1)S(1)}, u32[]{:S(2)}) copy-start(bf16[2,4,4,8,7296]{4,3,2,1,0:T(8,128)(2,1)S(1)} %pad_maximum_fusion) | copy-start | bytes 11206660
  76.1 2.1 %copy-start = (bf16[1,4,4,8,7296]{4,3,2,1,0:T(8,128)(2,1)S(1)}, bf16[1,4,4,8,7296]{4,3,2,1,0:T(8,128)(2,1)}, u32[]{:S(2)}) copy-start(bf16[1,4,4,8,7296]{4,3,2,1,0:T(8,128)(2,1)} %get-tuple-element.16) | copy-start | bytes 5603332
  77.8 20.8 %collective-permute-start.7 = (bf16[128,7168]{1,0:T(8,128)(2,1)S(1)}, bf16[128,7168]{1,0:T(8,128)(2,1)}, u32[]{:S(2)}, u32[]{:S(2)}) collective-permute-start(bf16[128,7168]{1,0:T(8,128)(2,1)S(1)} %slice.125), channel_id=1, source_target_pairs={{0,1},{1,0},{2,3},{3,2},{4,5},{5,4},{6,7},{7,6},{8,9},{9,8},{10,11... | collective-permute-start | bytes 5505032 | tf_op jit(solution)/shard_map/ppermute | solution.py:21
  80.0 1.8 %copy-start.1 = (bf16[2,4,4,8,7296]{4,3,2,1,0:T(8,128)(2,1)}, bf16[2,4,4,8,7296]{4,3,2,1,0:T(8,128)(2,1)S(1)}, u32[]{:S(2)}) copy-start(bf16[2,4,4,8,7296]{4,3,2,1,0:T(8,128)(2,1)S(1)} %pad_maximum_fusion.1) | copy-start | bytes 11206660
  96.4 2.6 %copy-start.3 = (bf16[256,7168]{1,0:T(8,128)(2,1)S(1)}, bf16[256,7168]{1,0:T(8,128)(2,1)}, u32[]{:S(2)}) copy-start(bf16[256,7168]{1,0:T(8,128)(2,1)} %fusion.5) | copy-start | bytes 11010052
  98.2 5.9 %collective-permute-start.23 = (bf16[128,7168]{1,0:T(8,128)(2,1)S(1)}, bf16[128,7168]{1,0:T(8,128)(2,1)S(1)}, u32[]{:S(2)}, u32[]{:S(2)}) collective-permute-start(bf16[128,7168]{1,0:T(8,128)(2,1)S(1)} %slice.139), channel_id=1, source_target_pairs={{0,1},{1,0},{2,3},{3,2},{4,5},{5,4},{6,7},{7,6},{8,9},{9,8},{10,11... | collective-permute-start | bytes 5505032 | tf_op jit(solution)/shard_map/ppermute | solution.py:21
  99.0 5.0 %copy-start.4 = (bf16[256,7168]{1,0:T(8,128)(2,1)S(1)}, bf16[256,7168]{1,0:T(8,128)(2,1)}, u32[]{:S(2)}) copy-start(bf16[256,7168]{1,0:T(8,128)(2,1)} %fusion.2) | copy-start | bytes 11010052
  101.3 13.8 %collective-permute-start.10 = (bf16[4,8,7168]{2,1,0:T(8,128)(2,1)S(1)}, bf16[4,8,7168]{2,1,0:T(8,128)(2,1)S(1)}, u32[]{:S(2)}, u32[]{:S(2)}) collective-permute-start(bf16[4,8,7168]{2,1,0:T(8,128)(2,1)S(1)} %get-tuple-element.23), channel_id=1, source_target_pairs={{0,4},{1,17},{2,6},{3,19},{4,8},{5,21},{6,10},{7,23},{8,12},{9,25}... | collective-permute-start | bytes 1376264 | tf_op jit(solution)/shard_map/ppermute | solution.py:21
  101.4 13.7 %collective-permute-start.9 = (bf16[4,8,7168]{2,1,0:T(8,128)(2,1)S(1)}, bf16[4,8,7168]{2,1,0:T(8,128)(2,1)S(1)}, u32[]{:S(2)}, u32[]{:S(2)}) collective-permute-start(bf16[4,8,7168]{2,1,0:T(8,128)(2,1)S(1)} %get-tuple-element.24), channel_id=1, source_target_pairs={{0,8},{1,33},{2,10},{3,35},{4,12},{5,37},{6,14},{7,39},{8,0},{9,41... | collective-permute-start | bytes 1376264 | tf_op jit(solution)/shard_map/ppermute | solution.py:21
  102.7 13.1 %collective-permute-start.8 = (bf16[4,8,7168]{2,1,0:T(8,128)(2,1)S(1)}, bf16[4,8,7168]{2,1,0:T(8,128)(2,1)S(1)}, u32[]{:S(2)}, u32[]{:S(2)}) collective-permute-start(bf16[4,8,7168]{2,1,0:T(8,128)(2,1)S(1)} %get-tuple-element.22), channel_id=1, source_target_pairs={{0,12},{1,49},{2,14},{3,51},{4,0},{5,53},{6,2},{7,55},{8,4},{9,57}... | collective-permute-start | bytes 1376264 | tf_op jit(solution)/shard_map/ppermute | solution.py:21
  104.7 22.1 %collective-permute-start.26 = (bf16[4,8,7168]{2,1,0:T(8,128)(2,1)S(1)}, bf16[4,8,7168]{2,1,0:T(8,128)(2,1)S(1)}, u32[]{:S(2)}, u32[]{:S(2)}) collective-permute-start(bf16[4,8,7168]{2,1,0:T(8,128)(2,1)S(1)} %get-tuple-element.20), channel_id=1, source_target_pairs={{0,4},{1,17},{2,6},{3,19},{4,8},{5,21},{6,10},{7,23},{8,12},{9,25}... | collective-permute-start | bytes 1376264 | tf_op jit(solution)/shard_map/ppermute | solution.py:21
  105.4 22.5 %collective-permute-start.25 = (bf16[4,8,7168]{2,1,0:T(8,128)(2,1)S(1)}, bf16[4,8,7168]{2,1,0:T(8,128)(2,1)S(1)}, u32[]{:S(2)}, u32[]{:S(2)}) collective-permute-start(bf16[4,8,7168]{2,1,0:T(8,128)(2,1)S(1)} %get-tuple-element.21), channel_id=1, source_target_pairs={{0,8},{1,33},{2,10},{3,35},{4,12},{5,37},{6,14},{7,39},{8,0},{9,41... | collective-permute-start | bytes 1376264 | tf_op jit(solution)/shard_map/ppermute | solution.py:21
  115.1 12.7 %collective-permute-start.24 = (bf16[4,8,7168]{2,1,0:T(8,128)(2,1)S(1)}, bf16[4,8,7168]{2,1,0:T(8,128)(2,1)S(1)}, u32[]{:S(2)}, u32[]{:S(2)}) collective-permute-start(bf16[4,8,7168]{2,1,0:T(8,128)(2,1)S(1)} %get-tuple-element.19), channel_id=1, source_target_pairs={{0,12},{1,49},{2,14},{3,51},{4,0},{5,53},{6,2},{7,55},{8,4},{9,57}... | collective-permute-start | bytes 1376264 | tf_op jit(solution)/shard_map/ppermute | solution.py:21
  115.8 15.4 %copy-start.5 = (bf16[1,8,7168]{2,1,0:T(8,128)(2,1)S(1)}, bf16[1,8,7168]{2,1,0:T(8,128)(2,1)}, u32[]{:S(2)}) copy-start(bf16[1,8,7168]{2,1,0:T(8,128)(2,1)} %param.6) | copy-start | bytes 344068
  116.0 13.4 %collective-permute-start.13 = (bf16[8,7168]{1,0:T(8,128)(2,1)S(1)}, bf16[8,7168]{1,0:T(8,128)(2,1)S(1)}, u32[]{:S(2)}, u32[]{:S(2)}) collective-permute-start(bf16[8,7168]{1,0:T(8,128)(2,1)S(1)} %get-tuple-element.33), channel_id=1, source_target_pairs={{0,16},{1,5},{2,18},{3,7},{4,20},{5,9},{6,22},{7,11},{8,24},{9,13}... | collective-permute-start | bytes 344072 | tf_op jit(solution)/shard_map/ppermute | solution.py:21
  116.1 15.0 %collective-permute-start.12 = (bf16[8,7168]{1,0:T(8,128)(2,1)S(1)}, bf16[8,7168]{1,0:T(8,128)(2,1)S(1)}, u32[]{:S(2)}, u32[]{:S(2)}) collective-permute-start(bf16[8,7168]{1,0:T(8,128)(2,1)S(1)} %get-tuple-element.34), channel_id=1, source_target_pairs={{0,32},{1,9},{2,34},{3,11},{4,36},{5,13},{6,38},{7,15},{8,40},{9,1... | collective-permute-start | bytes 344072 | tf_op jit(solution)/shard_map/ppermute | solution.py:21
  126.8 4.3 %collective-permute-start.11 = (bf16[8,7168]{1,0:T(8,128)(2,1)S(1)}, bf16[8,7168]{1,0:T(8,128)(2,1)S(1)}, u32[]{:S(2)}, u32[]{:S(2)}) collective-permute-start(bf16[8,7168]{1,0:T(8,128)(2,1)S(1)} %get-tuple-element.32), channel_id=1, source_target_pairs={{0,48},{1,13},{2,50},{3,15},{4,52},{5,1},{6,54},{7,3},{8,56},{9,5}... | collective-permute-start | bytes 344072 | tf_op jit(solution)/shard_map/ppermute | solution.py:21
  128.1 6.2 %collective-permute-start.29 = (bf16[8,7168]{1,0:T(8,128)(2,1)S(1)}, bf16[8,7168]{1,0:T(8,128)(2,1)S(1)}, u32[]{:S(2)}, u32[]{:S(2)}) collective-permute-start(bf16[8,7168]{1,0:T(8,128)(2,1)S(1)} %get-tuple-element.30), channel_id=1, source_target_pairs={{0,16},{1,5},{2,18},{3,7},{4,20},{5,9},{6,22},{7,11},{8,24},{9,13}... | collective-permute-start | bytes 344072 | tf_op jit(solution)/shard_map/ppermute | solution.py:21
  128.6 5.7 %collective-permute-start.28 = (bf16[8,7168]{1,0:T(8,128)(2,1)S(1)}, bf16[8,7168]{1,0:T(8,128)(2,1)S(1)}, u32[]{:S(2)}, u32[]{:S(2)}) collective-permute-start(bf16[8,7168]{1,0:T(8,128)(2,1)S(1)} %get-tuple-element.31), channel_id=1, source_target_pairs={{0,32},{1,9},{2,34},{3,11},{4,36},{5,13},{6,38},{7,15},{8,40},{9,1... | collective-permute-start | bytes 344072 | tf_op jit(solution)/shard_map/ppermute | solution.py:21
  129.4 5.8 %collective-permute-start.27 = (bf16[8,7168]{1,0:T(8,128)(2,1)S(1)}, bf16[8,7168]{1,0:T(8,128)(2,1)S(1)}, u32[]{:S(2)}, u32[]{:S(2)}) collective-permute-start(bf16[8,7168]{1,0:T(8,128)(2,1)S(1)} %get-tuple-element.29), channel_id=1, source_target_pairs={{0,48},{1,13},{2,50},{3,15},{4,52},{5,1},{6,54},{7,3},{8,56},{9,5}... | collective-permute-start | bytes 344072 | tf_op jit(solution)/shard_map/ppermute | solution.py:21
  131.2 9.0 %collective-permute-start.14 = (f32[8,7168]{1,0:T(8,128)S(1)}, f32[8,7168]{1,0:T(8,128)S(1)}, u32[]{:S(2)}, u32[]{:S(2)}) collective-permute-start(f32[8,7168]{1,0:T(8,128)S(1)} %fusion.29), channel_id=1, source_target_pairs={{0,64},{1,65},{2,66},{3,67},{4,68},{5,69},{6,70},{7,71},{8,72},{9,... | collective-permute-start | bytes 688136 | tf_op jit(solution)/shard_map/ppermute | solution.py:125
  135.3 14.4 %collective-permute-start.30 = (bf16[8,7168]{1,0:T(8,128)(2,1)S(1)}, bf16[8,7168]{1,0:T(8,128)(2,1)S(1)}, u32[]{:S(2)}, u32[]{:S(2)}) collective-permute-start(bf16[8,7168]{1,0:T(8,128)(2,1)S(1)} %fusion.25), channel_id=1, source_target_pairs={{0,66},{1,67},{2,64},{3,65},{4,70},{5,71},{6,68},{7,69},{8,74},{9,... | collective-permute-start | bytes 344072 | tf_op jit(solution)/shard_map/ppermute | solution.py:126

commit v3 on v2

--- a/solution.py
+++ b/solution.py
@@ -102,6 +102,8 @@
         sent = summed.astype(jnp.bfloat16)
         for m in range(1, ring):
             total = total + moved(sent[m], along(1, -m)).astype(jnp.float32)
+        if after is not None:
+            return total, part
         result = total[0]
         sent = total.astype(jnp.bfloat16)
         for k in range(1, ring):
@@ -114,17 +116,20 @@
 
     mine = tokens.astype(jnp.float32) + own_sum
     theirs = partner_sum.astype(jnp.bfloat16)
+    ahead_of = lambda k: (lambda e: across_z(*coords(along(0, -k)(*coords(e)))))
     sections = lax.axis_size("segment")
     count = X_SIZE * Y_SIZE * Z_SIZE * C_SIZE
     relay = [(s * count + e, (s + 1) % sections * count + e) for s in range(sections) for e in range(count)]
-    cross = [
-        (s * count + e, (s + 1) % sections * count + across_z(*coords(e)))
-        for s in range(sections)
-        for e in range(count)
-    ]
     got_mine = lax.ppermute(mine, ("segment", "expert"), relay)
-    got_theirs = lax.ppermute(theirs, ("segment", "expert"), cross)
-    next_input = (got_mine + got_theirs.astype(jnp.float32)).astype(jnp.bfloat16)
+    got = got_mine
+    for k in range(ring):
+        pairs = [
+            (s * count + e, (s + 1) % sections * count + ahead_of(k)(e))
+            for s in range(sections)
+            for e in range(count)
+        ]
+        got = got + lax.ppermute(theirs[k], ("segment", "expert"), pairs).astype(jnp.float32)
+    next_input = got.astype(jnp.bfloat16)
     return next_input[None]
 
 

time: 151 us -> 172 us (1.14)
  the two profiles are of different devices: /device:TPU:65 before, /device:TPU:1 now
where the time goes in v3:
time: 172 us
  waiting for transfers between devices  64.9 us (38%)
  starting transfers between devices  54.9 us (32%)
  matrix products  28.8 us (17%)
  other arithmetic  14.7 us (9%)
  local copies, waits for them, and re-layouts  8.23 us (5%)
    ppermute x26, starting transfers between devices, moved(): return lax.ppermute(value, 'expert', pairs)  43.1 us
    ppermute x26, waiting for transfers between devices, moved(): return lax.ppermute(value, 'expert', pairs)  40.8 us
    ppermute x4, waiting for transfers between devices, layer(): lax.ppermute(theirs[k], ('segment', 'expert'), pairs).astype(jnp.float32)  24 us
    dot_general x2, matrix products, expert_rows(): part = jnp.dot(hidden, down_mat, preferred_element_type=jnp.float32)  20.2 us
    ppermute x4, starting transfers between devices, layer(): lax.ppermute(theirs[k], ('segment', 'expert'), pairs).astype(jnp.float32)  11.1 us
    dot_general x2, matrix products, expert_rows(): upper_act = jnp.dot(rows, upper_mat, preferred_element_type=jnp.float32)  8.61 us
    another operation x4, other arithmetic, served(): jnp.stack([first] + [moved(first, along(1, k)) for k in range(1, ring)])  5.16 us
    unnamed x13, local copies, waits for them, and re-layouts  4.34 us
  transfers between devices with their start and end apart: 31, of which 16 were waited for; matrix products, arithmetic and copies ran while one was open for 26% of the time, Pallas kernels for 0%

profile of v3, /device:TPU:1, one launch (start us, length us, event | category | flops | bytes accessed | tf_op | source)
XLA Modules:
  0.0 171.7 jit_solution(1987077048318423106)
XLA Ops:
  0.0 0.8 select_reduce_fusion
  0.9 0.9 fusion.56
  1.8 2.2 %collective-permute-start = (bf16[8,7296]{1,0:T(8,128)(2,1)S(1)}, bf16[8,7296]{1,0:T(8,128)(2,1)S(1)}, u32[]{:S(2)}, u32[]{:S(2)}) collective-permute-start(bf16[8,7296]{1,0:T(8,128)(2,1)S(1)} %get-tuple-element.35), channel_id=1, source_target_pairs={{0,16},{1,5},{2,18},{3,7},{4,20},{5,9},{6,22},{7,11},{8,24},{9,13}... | collective-permute-start | bytes 350216 | tf_op jit(solution)/shard_map/ppermute | solution.py:21
  4.0 2.6 %collective-permute-start.1 = (bf16[8,7296]{1,0:T(8,128)(2,1)S(1)}, bf16[8,7296]{1,0:T(8,128)(2,1)S(1)}, u32[]{:S(2)}, u32[]{:S(2)}) collective-permute-start(bf16[8,7296]{1,0:T(8,128)(2,1)S(1)} %get-tuple-element.35), channel_id=1, source_target_pairs={{0,32},{1,9},{2,34},{3,11},{4,36},{5,13},{6,38},{7,15},{8,40},{9,1... | collective-permute-start | bytes 350216 | tf_op jit(solution)/shard_map/ppermute | solution.py:21
  6.6 1.1 collective-permute-start.2
  7.7 2.7 %collective-permute-done.1 = bf16[8,7296]{1,0:T(8,128)(2,1)S(1)} collective-permute-done((bf16[8,7296]{1,0:T(8,128)(2,1)S(1)}, bf16[8,7296]{1,0:T(8,128)(2,1)S(1)}, u32[]{:S(2)}, u32[]{:S(2)}) %collective-permute-start.1) | collective-permute-done | bytes 116768 | tf_op jit(solution)/shard_map/ppermute | solution.py:21
  10.7 2.6 %collective-permute-start.5 = (bf16[4,8,7296]{2,1,0:T(8,128)(2,1)S(1)}, bf16[4,8,7296]{2,1,0:T(8,128)(2,1)S(1)}, u32[]{:S(2)}, u32[]{:S(2)}) collective-permute-start(bf16[4,8,7296]{2,1,0:T(8,128)(2,1)S(1)} %get-tuple-element.24), channel_id=1, source_target_pairs={{0,12},{1,49},{2,14},{3,51},{4,0},{5,53},{6,2},{7,55},{8,4},{9,57}... | collective-permute-start | bytes 1400840 | tf_op jit(solution)/shard_map/ppermute | solution.py:21
  13.2 1.7 %collective-permute-start.4 = (bf16[4,8,7296]{2,1,0:T(8,128)(2,1)S(1)}, bf16[4,8,7296]{2,1,0:T(8,128)(2,1)S(1)}, u32[]{:S(2)}, u32[]{:S(2)}) collective-permute-start(bf16[4,8,7296]{2,1,0:T(8,128)(2,1)S(1)} %get-tuple-element.24), channel_id=1, source_target_pairs={{0,8},{1,33},{2,10},{3,35},{4,12},{5,37},{6,14},{7,39},{8,0},{9,41... | collective-permute-start | bytes 1400840 | tf_op jit(solution)/shard_map/ppermute | solution.py:21
  15.0 6.9 %collective-permute-start.15 = (bf16[8,7296]{1,0:T(8,128)(2,1)S(1)}, bf16[8,7296]{1,0:T(8,128)(2,1)S(1)}, u32[]{:S(2)}, u32[]{:S(2)}) collective-permute-start(bf16[8,7296]{1,0:T(8,128)(2,1)S(1)} %get-tuple-element.35), channel_id=1, source_target_pairs={{0,2},{1,3},{2,0},{3,1},{4,6},{5,7},{6,4},{7,5},{8,10},{9,11},{10,... | collective-permute-start | bytes 350216 | tf_op jit(solution)/shard_map/ppermute | solution.py:21
  21.9 2.3 %collective-permute-done.15 = bf16[8,7296]{1,0:T(8,128)(2,1)S(1)} collective-permute-done((bf16[8,7296]{1,0:T(8,128)(2,1)S(1)}, bf16[8,7296]{1,0:T(8,128)(2,1)S(1)}, u32[]{:S(2)}, u32[]{:S(2)}) %collective-permute-start.15) | collective-permute-done | bytes 116768 | tf_op jit(solution)/shard_map/ppermute | solution.py:21
  24.9 2.6 %collective-permute-start.17 = (bf16[8,7296]{1,0:T(8,128)(2,1)S(1)}, bf16[8,7296]{1,0:T(8,128)(2,1)S(1)}, u32[]{:S(2)}, u32[]{:S(2)}) collective-permute-start(bf16[8,7296]{1,0:T(8,128)(2,1)S(1)} %collective-permute-done.15), channel_id=1, source_target_pairs={{0,32},{1,9},{2,34},{3,11},{4,36},{5,13},{6,38},{7,15},{8,40},{9,1... | collective-permute-start | bytes 350216 | tf_op jit(solution)/shard_map/ppermute | solution.py:21
  27.5 0.8 collective-permute-start.18
  28.3 1.6 pad_maximum_fusion.2
  29.9 5.3 %collective-permute-start.6 = (bf16[4,4,8,7296]{3,2,1,0:T(8,128)(2,1)}, bf16[4,4,8,7296]{3,2,1,0:T(8,128)(2,1)}, u32[]{:S(2)}, u32[]{:S(2)}) collective-permute-start(bf16[4,4,8,7296]{3,2,1,0:T(8,128)(2,1)} %get-tuple-element.13), channel_id=1, source_target_pairs={{0,1},{1,0},{2,3},{3,2},{4,5},{5,4},{6,7},{7,6},{8,9},{9,8},{10,11... | collective-permute-start | bytes 5603336 | tf_op jit(solution)/shard_map/ppermute | solution.py:21
  35.3 0.9 collective-permute-start.19
  36.2 1.7 collective-permute-start.20
  37.9 0.8 collective-permute-start.21
  38.7 10.7 %collective-permute-done.19 = bf16[4,8,7296]{2,1,0:T(8,128)(2,1)S(1)} collective-permute-done((bf16[4,8,7296]{2,1,0:T(8,128)(2,1)S(1)}, bf16[4,8,7296]{2,1,0:T(8,128)(2,1)S(1)}, u32[]{:S(2)}, u32[]{:S(2)}) %collective-permute-start.19) | collective-permute-done | bytes 466976 | tf_op jit(solution)/shard_map/ppermute | solution.py:21
  50.0 3.4 %pad_maximum_fusion.3 = (bf16[4,4,8,7296]{3,2,1,0:T(8,128)(2,1)}, bf16[1,4,4,8,7296]{4,3,2,1,0:T(8,128)(2,1)}) fusion(bf16[1,4,8,7296]{3,2,1,0:T(8,128)(2,1)} %bitcast.33, bf16[1,4,8,7296]{3,2,1,0:T(8,128)(2,1)} %bitcast.32, bf16[1,4,8,7296]{3,2,1,0:T(8,128)(2,1)S(1)} %bitcast.107, bf16[1,4,8,7296]{3,2,1,0:T(8,128)(2,1)S(1)} %get-tuple-element.25), kind=kLoop, calls=%fused_computation.23 | loop fusion | flops 2801664 | bytes 5603328 | tf_op jit(solution)/shard_map/stack | solution.py:89
  53.4 3.4 %collective-permute-start.22 = (bf16[4,4,8,7296]{3,2,1,0:T(8,128)(2,1)}, bf16[4,4,8,7296]{3,2,1,0:T(8,128)(2,1)}, u32[]{:S(2)}, u32[]{:S(2)}) collective-permute-start(bf16[4,4,8,7296]{3,2,1,0:T(8,128)(2,1)} %get-tuple-element.15), channel_id=1, source_target_pairs={{0,1},{1,0},{2,3},{3,2},{4,5},{5,4},{6,7},{7,6},{8,9},{9,8},{10,11... | collective-permute-start | bytes 5603336 | tf_op jit(solution)/shard_map/ppermute | solution.py:21
  56.8 1.9 %pad_maximum_fusion = bf16[2,4,4,8,7296]{4,3,2,1,0:T(8,128)(2,1)S(1)} fusion(bf16[1,4,4,8,7296]{4,3,2,1,0:T(8,128)(2,1)S(1)} %get-tuple-element.14, bf16[1,4,4,8,7296]{4,3,2,1,0:T(8,128)(2,1)} %bitcast.11), kind=kLoop, calls=%fused_computation.8 | loop fusion | flops 1867776 | bytes 7471104 | tf_op jit(solution)/shard_map/stack | solution.py:91
  58.7 1.8 %copy-done.2 = bf16[2,4,4,8,7296]{4,3,2,1,0:T(8,128)(2,1)} copy-done((bf16[2,4,4,8,7296]{4,3,2,1,0:T(8,128)(2,1)}, bf16[2,4,4,8,7296]{4,3,2,1,0:T(8,128)(2,1)S(1)}, u32[]{:S(2)}) %copy-start.2) | copy-done | bytes 3735576
  60.7 4.3 %fusion.10 = f32[256,256]{1,0:T(8,128)S(1)} fusion(bf16[256,7296]{1,0:T(8,128)(2,1)} %bitcast.105, bf16[7168,256]{1,0:T(8,128)(2,1)} %bitcast.123), kind=kOutput, calls=%fused_computation.16 | convolution fusion | flops 956301312 | bytes 7667712 | tf_op jit(solution)/shard_map/dot_general | solution.py:44
  65.0 10.0 %fusion.5 = bf16[256,7168]{1,0:T(8,128)(2,1)} fusion(bf16[1,1,256,7168]{3,2,1,0:T(8,128)(2,1)} %param.11, f32[256]{0:T(256)S(1)} %bitcast.122, f32[256,256]{1,0:T(8,128)S(1)} %fusion.10, bf16[256,7296]{1,0:T(8,128)(2,1)} %bitcast.106, bf16[7168,256]{1,0:T(8,128)(2,1)} %bitcast.125), kind=kOutput, calls=%fused_computation.7 | convolution fusion | flops 1903558656 | bytes 15008768 | tf_op jit(solution)/shard_map/dot_general | solution.py:46
  75.0 1.8 %slice.125 = bf16[128,7168]{1,0:T(8,128)(2,1)S(1)} slice(bf16[256,7168]{1,0:T(8,128)(2,1)} %fusion.5), slice={[0:128], [0:7168]} | slice | bytes 3670016 | tf_op jit(solution)/shard_map/slice | solution.py:98
  77.1 1.9 %pad_maximum_fusion.1 = bf16[2,4,4,8,7296]{4,3,2,1,0:T(8,128)(2,1)S(1)} fusion(bf16[1,4,4,8,7296]{4,3,2,1,0:T(8,128)(2,1)S(1)} %copy-done, bf16[1,4,4,8,7296]{4,3,2,1,0:T(8,128)(2,1)} %bitcast.34), kind=kLoop, calls=%fused_computation.9 | loop fusion | flops 1867776 | bytes 7471104 | tf_op jit(solution)/shard_map/stack | solution.py:91
  79.0 1.8 %copy-done.1 = bf16[2,4,4,8,7296]{4,3,2,1,0:T(8,128)(2,1)} copy-done((bf16[2,4,4,8,7296]{4,3,2,1,0:T(8,128)(2,1)}, bf16[2,4,4,8,7296]{4,3,2,1,0:T(8,128)(2,1)S(1)}, u32[]{:S(2)}) %copy-start.1) | copy-done | bytes 3735576
  81.0 4.3 %fusion.8 = f32[256,256]{1,0:T(8,128)S(1)} fusion(bf16[256,7296]{1,0:T(8,128)(2,1)} %bitcast.102, bf16[7168,256]{1,0:T(8,128)(2,1)} %bitcast.124), kind=kOutput, calls=%fused_computation.14 | convolution fusion | flops 956301312 | bytes 7667712 | tf_op jit(solution)/shard_map/dot_general | solution.py:44
  85.3 10.1 %fusion.2 = bf16[256,7168]{1,0:T(8,128)(2,1)} fusion(bf16[1,1,256,7168]{3,2,1,0:T(8,128)(2,1)} %param.11, f32[256]{0:T(256)S(1)} %bitcast.121, f32[256,256]{1,0:T(8,128)S(1)} %fusion.8, bf16[256,7296]{1,0:T(8,128)(2,1)} %bitcast.103, bf16[7168,256]{1,0:T(8,128)(2,1)} %bitcast.126), kind=kOutput, calls=%fused_computation.3 | convolution fusion | flops 1903558656 | bytes 15008768 | tf_op jit(solution)/shard_map/dot_general | solution.py:46
  95.4 1.8 %slice.139 = bf16[128,7168]{1,0:T(8,128)(2,1)S(1)} slice(bf16[256,7168]{1,0:T(8,128)(2,1)} %fusion.2), slice={[0:128], [0:7168]} | slice | bytes 3670016 | tf_op jit(solution)/shard_map/slice | solution.py:98
  98.0 2.2 %convert_add_fusion.1 = (f32[128,7168]{1,0:T(8,128)S(1)}, bf16[128,7168]{1,0:T(8,128)(2,1)S(1)}) fusion(bf16[128,7168]{1,0:T(8,128)(2,1)} %collective-permute-done.7, bf16[256,7168]{1,0:T(8,128)(2,1)S(1)} %copy-done.3), kind=kLoop, calls=%fused_computation.13 | loop fusion | flops 3670016 | bytes 9175040 | tf_op jit(solution)/shard_map/add | solution.py:99
  100.9 2.1 %collective-permute-start.8 = (bf16[4,8,7168]{2,1,0:T(8,128)(2,1)S(1)}, bf16[4,8,7168]{2,1,0:T(8,128)(2,1)S(1)}, u32[]{:S(2)}, u32[]{:S(2)}) collective-permute-start(bf16[4,8,7168]{2,1,0:T(8,128)(2,1)S(1)} %get-tuple-element.17), channel_id=1, source_target_pairs={{0,12},{1,49},{2,14},{3,51},{4,0},{5,53},{6,2},{7,55},{8,4},{9,57}... | collective-permute-start | bytes 1376264 | tf_op jit(solution)/shard_map/ppermute | solution.py:21
  104.0 5.3 %collective-permute-done.10 = bf16[4,8,7168]{2,1,0:T(8,128)(2,1)S(1)} collective-permute-done((bf16[4,8,7168]{2,1,0:T(8,128)(2,1)S(1)}, bf16[4,8,7168]{2,1,0:T(8,128)(2,1)S(1)}, u32[]{:S(2)}, u32[]{:S(2)}) %collective-permute-start.10) | collective-permute-done | bytes 458784 | tf_op jit(solution)/shard_map/ppermute | solution.py:21
  109.2 4.2 %collective-permute-done.8 = bf16[4,8,7168]{2,1,0:T(8,128)(2,1)S(1)} collective-permute-done((bf16[4,8,7168]{2,1,0:T(8,128)(2,1)S(1)}, bf16[4,8,7168]{2,1,0:T(8,128)(2,1)S(1)}, u32[]{:S(2)}, u32[]{:S(2)}) %collective-permute-start.8) | collective-permute-done | bytes 458784 | tf_op jit(solution)/shard_map/ppermute | solution.py:21
  113.4 1.1 collective-permute-done.9
  114.7 2.4 %collective-permute-start.11 = (bf16[8,7168]{1,0:T(8,128)(2,1)S(1)}, bf16[8,7168]{1,0:T(8,128)(2,1)S(1)}, u32[]{:S(2)}, u32[]{:S(2)}) collective-permute-start(bf16[8,7168]{1,0:T(8,128)(2,1)S(1)} %get-tuple-element.31), channel_id=1, source_target_pairs={{0,48},{1,13},{2,50},{3,15},{4,52},{5,1},{6,54},{7,3},{8,56},{9,5}... | collective-permute-start | bytes 344072 | tf_op jit(solution)/shard_map/ppermute | solution.py:21
  117.9 2.4 %collective-permute-start.24 = (bf16[4,8,7168]{2,1,0:T(8,128)(2,1)S(1)}, bf16[4,8,7168]{2,1,0:T(8,128)(2,1)S(1)}, u32[]{:S(2)}, u32[]{:S(2)}) collective-permute-start(bf16[4,8,7168]{2,1,0:T(8,128)(2,1)S(1)} %get-tuple-element.20), channel_id=1, source_target_pairs={{0,12},{1,49},{2,14},{3,51},{4,0},{5,53},{6,2},{7,55},{8,4},{9,57}... | collective-permute-start | bytes 1376264 | tf_op jit(solution)/shard_map/ppermute | solution.py:21
  121.0 1.4 collective-permute-done.12
  122.4 1.4 collective-permute-done.13
  124.5 7.0 %collective-permute-done.24 = bf16[4,8,7168]{2,1,0:T(8,128)(2,1)S(1)} collective-permute-done((bf16[4,8,7168]{2,1,0:T(8,128)(2,1)S(1)}, bf16[4,8,7168]{2,1,0:T(8,128)(2,1)S(1)}, u32[]{:S(2)}, u32[]{:S(2)}) %collective-permute-start.24) | collective-permute-done | bytes 458784 | tf_op jit(solution)/shard_map/ppermute | solution.py:21
  131.6 4.0 %collective-permute-done.26 = bf16[4,8,7168]{2,1,0:T(8,128)(2,1)S(1)} collective-permute-done((bf16[4,8,7168]{2,1,0:T(8,128)(2,1)S(1)}, bf16[4,8,7168]{2,1,0:T(8,128)(2,1)S(1)}, u32[]{:S(2)}, u32[]{:S(2)}) %collective-permute-start.26) | collective-permute-done | bytes 458784 | tf_op jit(solution)/shard_map/ppermute | solution.py:21
  135.8 5.5 %collective-permute-start.27 = (bf16[8,7168]{1,0:T(8,128)(2,1)S(1)}, bf16[8,7168]{1,0:T(8,128)(2,1)S(1)}, u32[]{:S(2)}, u32[]{:S(2)}) collective-permute-start(bf16[8,7168]{1,0:T(8,128)(2,1)S(1)} %get-tuple-element.27), channel_id=1, source_target_pairs={{0,66},{1,67},{2,64},{3,65},{4,70},{5,71},{6,68},{7,69},{8,74},{9,... | collective-permute-start | bytes 344072 | tf_op jit(solution)/shard_map/ppermute | solution.py:131
  141.3 1.6 collective-permute-start.28
  142.9 3.8 %collective-permute-start.29 = (bf16[8,7168]{1,0:T(8,128)(2,1)S(1)}, bf16[8,7168]{1,0:T(8,128)(2,1)S(1)}, u32[]{:S(2)}, u32[]{:S(2)}) collective-permute-start(bf16[8,7168]{1,0:T(8,128)(2,1)S(1)} %get-tuple-element.29), channel_id=1, source_target_pairs={{0,98},{1,75},{2,96},{3,73},{4,102},{5,79},{6,100},{7,77},{8,106},... | collective-permute-start | bytes 344072 | tf_op jit(solution)/shard_map/ppermute | solution.py:131
  146.9 16.7 %collective-permute-done.27 = bf16[8,7168]{1,0:T(8,128)(2,1)S(1)} collective-permute-done((bf16[8,7168]{1,0:T(8,128)(2,1)S(1)}, bf16[8,7168]{1,0:T(8,128)(2,1)S(1)}, u32[]{:S(2)}, u32[]{:S(2)}) %collective-permute-start.27) | collective-permute-done | bytes 114720 | tf_op jit(solution)/shard_map/ppermute | solution.py:131
  163.6 2.5 %collective-permute-done.28 = bf16[8,7168]{1,0:T(8,128)(2,1)S(1)} collective-permute-done((bf16[8,7168]{1,0:T(8,128)(2,1)S(1)}, bf16[8,7168]{1,0:T(8,128)(2,1)S(1)}, u32[]{:S(2)}, u32[]{:S(2)}) %collective-permute-start.28) | collective-permute-done | bytes 114720 | tf_op jit(solution)/shard_map/ppermute | solution.py:131
  166.0 2.5 %collective-permute-done.29 = bf16[8,7168]{1,0:T(8,128)(2,1)S(1)} collective-permute-done((bf16[8,7168]{1,0:T(8,128)(2,1)S(1)}, bf16[8,7168]{1,0:T(8,128)(2,1)S(1)}, u32[]{:S(2)}, u32[]{:S(2)}) %collective-permute-start.29) | collective-permute-done | bytes 114720 | tf_op jit(solution)/shard_map/ppermute | solution.py:131
  168.5 2.5 %collective-permute-done.30 = bf16[8,7168]{1,0:T(8,128)(2,1)S(1)} collective-permute-done((bf16[8,7168]{1,0:T(8,128)(2,1)S(1)}, bf16[8,7168]{1,0:T(8,128)(2,1)S(1)}, u32[]{:S(2)}, u32[]{:S(2)}) %collective-permute-start.30) | collective-permute-done | bytes 114720 | tf_op jit(solution)/shard_map/ppermute | solution.py:131
  (60 shorter events, 8.4 us)
Async XLA Ops:
  1.8 5.9 %collective-permute-start = (bf16[8,7296]{1,0:T(8,128)(2,1)S(1)}, bf16[8,7296]{1,0:T(8,128)(2,1)S(1)}, u32[]{:S(2)}, u32[]{:S(2)}) collective-permute-start(bf16[8,7296]{1,0:T(8,128)(2,1)S(1)} %get-tuple-element.35), channel_id=1, source_target_pairs={{0,16},{1,5},{2,18},{3,7},{4,20},{5,9},{6,22},{7,11},{8,24},{9,13}... | collective-permute-start | bytes 350216 | tf_op jit(solution)/shard_map/ppermute | solution.py:21
  4.0 6.4 %collective-permute-start.1 = (bf16[8,7296]{1,0:T(8,128)(2,1)S(1)}, bf16[8,7296]{1,0:T(8,128)(2,1)S(1)}, u32[]{:S(2)}, u32[]{:S(2)}) collective-permute-start(bf16[8,7296]{1,0:T(8,128)(2,1)S(1)} %get-tuple-element.35), channel_id=1, source_target_pairs={{0,32},{1,9},{2,34},{3,11},{4,36},{5,13},{6,38},{7,15},{8,40},{9,1... | collective-permute-start | bytes 350216 | tf_op jit(solution)/shard_map/ppermute | solution.py:21
  6.6 4.0 %collective-permute-start.2 = (bf16[8,7296]{1,0:T(8,128)(2,1)S(1)}, bf16[8,7296]{1,0:T(8,128)(2,1)S(1)}, u32[]{:S(2)}, u32[]{:S(2)}) collective-permute-start(bf16[8,7296]{1,0:T(8,128)(2,1)S(1)} %get-tuple-element.35), channel_id=1, source_target_pairs={{0,48},{1,13},{2,50},{3,15},{4,52},{5,1},{6,54},{7,3},{8,56},{9,5}... | collective-permute-start | bytes 350216 | tf_op jit(solution)/shard_map/ppermute | solution.py:21
  10.7 16.8 %collective-permute-start.5 = (bf16[4,8,7296]{2,1,0:T(8,128)(2,1)S(1)}, bf16[4,8,7296]{2,1,0:T(8,128)(2,1)S(1)}, u32[]{:S(2)}, u32[]{:S(2)}) collective-permute-start(bf16[4,8,7296]{2,1,0:T(8,128)(2,1)S(1)} %get-tuple-element.24), channel_id=1, source_target_pairs={{0,12},{1,49},{2,14},{3,51},{4,0},{5,53},{6,2},{7,55},{8,4},{9,57}... | collective-permute-start | bytes 1400840 | tf_op jit(solution)/shard_map/ppermute | solution.py:21
  13.2 15.1 %collective-permute-start.3 = (bf16[4,8,7296]{2,1,0:T(8,128)(2,1)S(1)}, bf16[4,8,7296]{2,1,0:T(8,128)(2,1)S(1)}, u32[]{:S(2)}, u32[]{:S(2)}) collective-permute-start(bf16[4,8,7296]{2,1,0:T(8,128)(2,1)S(1)} %get-tuple-element.24), channel_id=1, source_target_pairs={{0,4},{1,17},{2,6},{3,19},{4,8},{5,21},{6,10},{7,23},{8,12},{9,25}... | collective-permute-start | bytes 1400840 | tf_op jit(solution)/shard_map/ppermute | solution.py:21
  13.2 15.1 %collective-permute-start.4 = (bf16[4,8,7296]{2,1,0:T(8,128)(2,1)S(1)}, bf16[4,8,7296]{2,1,0:T(8,128)(2,1)S(1)}, u32[]{:S(2)}, u32[]{:S(2)}) collective-permute-start(bf16[4,8,7296]{2,1,0:T(8,128)(2,1)S(1)} %get-tuple-element.24), channel_id=1, source_target_pairs={{0,8},{1,33},{2,10},{3,35},{4,12},{5,37},{6,14},{7,39},{8,0},{9,41... | collective-permute-start | bytes 1400840 | tf_op jit(solution)/shard_map/ppermute | solution.py:21
  15.0 9.2 %collective-permute-start.15 = (bf16[8,7296]{1,0:T(8,128)(2,1)S(1)}, bf16[8,7296]{1,0:T(8,128)(2,1)S(1)}, u32[]{:S(2)}, u32[]{:S(2)}) collective-permute-start(bf16[8,7296]{1,0:T(8,128)(2,1)S(1)} %get-tuple-element.35), channel_id=1, source_target_pairs={{0,2},{1,3},{2,0},{3,1},{4,6},{5,7},{6,4},{7,5},{8,10},{9,11},{10,... | collective-permute-start | bytes 350216 | tf_op jit(solution)/shard_map/ppermute | solution.py:21
  24.2 11.0 %collective-permute-start.16 = (bf16[8,7296]{1,0:T(8,128)(2,1)S(1)}, bf16[8,7296]{1,0:T(8,128)(2,1)S(1)}, u32[]{:S(2)}, u32[]{:S(2)}) collective-permute-start(bf16[8,7296]{1,0:T(8,128)(2,1)S(1)} %collective-permute-done.15), channel_id=1, source_target_pairs={{0,16},{1,5},{2,18},{3,7},{4,20},{5,9},{6,22},{7,11},{8,24},{9,13}... | collective-permute-start | bytes 350216 | tf_op jit(solution)/shard_map/ppermute | solution.py:21
  24.9 10.3 %collective-permute-start.17 = (bf16[8,7296]{1,0:T(8,128)(2,1)S(1)}, bf16[8,7296]{1,0:T(8,128)(2,1)S(1)}, u32[]{:S(2)}, u32[]{:S(2)}) collective-permute-start(bf16[8,7296]{1,0:T(8,128)(2,1)S(1)} %collective-permute-done.15), channel_id=1, source_target_pairs={{0,32},{1,9},{2,34},{3,11},{4,36},{5,13},{6,38},{7,15},{8,40},{9,1... | collective-permute-start | bytes 350216 | tf_op jit(solution)/shard_map/ppermute | solution.py:21
  27.5 7.7 %collective-permute-start.18 = (bf16[8,7296]{1,0:T(8,128)(2,1)S(1)}, bf16[8,7296]{1,0:T(8,128)(2,1)S(1)}, u32[]{:S(2)}, u32[]{:S(2)}) collective-permute-start(bf16[8,7296]{1,0:T(8,128)(2,1)S(1)} %collective-permute-done.15), channel_id=1, source_target_pairs={{0,48},{1,13},{2,50},{3,15},{4,52},{5,1},{6,54},{7,3},{8,56},{9,5}... | collective-permute-start | bytes 350216 | tf_op jit(solution)/shard_map/ppermute | solution.py:21
  29.9 26.9 %collective-permute-start.6 = (bf16[4,4,8,7296]{3,2,1,0:T(8,128)(2,1)}, bf16[4,4,8,7296]{3,2,1,0:T(8,128)(2,1)}, u32[]{:S(2)}, u32[]{:S(2)}) collective-permute-start(bf16[4,4,8,7296]{3,2,1,0:T(8,128)(2,1)} %get-tuple-element.13), channel_id=1, source_target_pairs={{0,1},{1,0},{2,3},{3,2},{4,5},{5,4},{6,7},{7,6},{8,9},{9,8},{10,11... | collective-permute-start | bytes 5603336 | tf_op jit(solution)/shard_map/ppermute | solution.py:21
  35.3 14.1 %collective-permute-start.19 = (bf16[4,8,7296]{2,1,0:T(8,128)(2,1)S(1)}, bf16[4,8,7296]{2,1,0:T(8,128)(2,1)S(1)}, u32[]{:S(2)}, u32[]{:S(2)}) collective-permute-start(bf16[4,8,7296]{2,1,0:T(8,128)(2,1)S(1)} %get-tuple-element.26), channel_id=1, source_target_pairs={{0,4},{1,17},{2,6},{3,19},{4,8},{5,21},{6,10},{7,23},{8,12},{9,25}... | collective-permute-start | bytes 1400840 | tf_op jit(solution)/shard_map/ppermute | solution.py:21
  36.2 13.2 %collective-permute-start.20 = (bf16[4,8,7296]{2,1,0:T(8,128)(2,1)S(1)}, bf16[4,8,7296]{2,1,0:T(8,128)(2,1)}, u32[]{:S(2)}, u32[]{:S(2)}) collective-permute-start(bf16[4,8,7296]{2,1,0:T(8,128)(2,1)S(1)} %get-tuple-element.26), channel_id=1, source_target_pairs={{0,8},{1,33},{2,10},{3,35},{4,12},{5,37},{6,14},{7,39},{8,0},{9,41... | collective-permute-start | bytes 1400840 | tf_op jit(solution)/shard_map/ppermute | solution.py:21
  37.9 12.1 %collective-permute-start.21 = (bf16[4,8,7296]{2,1,0:T(8,128)(2,1)S(1)}, bf16[4,8,7296]{2,1,0:T(8,128)(2,1)}, u32[]{:S(2)}, u32[]{:S(2)}) collective-permute-start(bf16[4,8,7296]{2,1,0:T(8,128)(2,1)S(1)} %get-tuple-element.26), channel_id=1, source_target_pairs={{0,12},{1,49},{2,14},{3,51},{4,0},{5,53},{6,2},{7,55},{8,4},{9,57}... | collective-permute-start | bytes 1400840 | tf_op jit(solution)/shard_map/ppermute | solution.py:21
  53.4 23.5 %collective-permute-start.22 = (bf16[4,4,8,7296]{3,2,1,0:T(8,128)(2,1)}, bf16[4,4,8,7296]{3,2,1,0:T(8,128)(2,1)}, u32[]{:S(2)}, u32[]{:S(2)}) collective-permute-start(bf16[4,4,8,7296]{3,2,1,0:T(8,128)(2,1)} %get-tuple-element.15), channel_id=1, source_target_pairs={{0,1},{1,0},{2,3},{3,2},{4,5},{5,4},{6,7},{7,6},{8,9},{9,8},{10,11... | collective-permute-start | bytes 5603336 | tf_op jit(solution)/shard_map/ppermute | solution.py:21
  58.7 1.8 %copy-start.2 = (bf16[2,4,4,8,7296]{4,3,2,1,0:T(8,128)(2,1)}, bf16[2,4,4,8,7296]{4,3,2,1,0:T(8,128)(2,1)S(1)}, u32[]{:S(2)}) copy-start(bf16[2,4,4,8,7296]{4,3,2,1,0:T(8,128)(2,1)S(1)} %pad_maximum_fusion) | copy-start | bytes 11206660
  75.0 2.1 %copy-start = (bf16[1,4,4,8,7296]{4,3,2,1,0:T(8,128)(2,1)S(1)}, bf16[1,4,4,8,7296]{4,3,2,1,0:T(8,128)(2,1)}, u32[]{:S(2)}) copy-start(bf16[1,4,4,8,7296]{4,3,2,1,0:T(8,128)(2,1)} %get-tuple-element.16) | copy-start | bytes 5603332
  76.8 20.8 %collective-permute-start.7 = (bf16[128,7168]{1,0:T(8,128)(2,1)S(1)}, bf16[128,7168]{1,0:T(8,128)(2,1)}, u32[]{:S(2)}, u32[]{:S(2)}) collective-permute-start(bf16[128,7168]{1,0:T(8,128)(2,1)S(1)} %slice.125), channel_id=1, source_target_pairs={{0,1},{1,0},{2,3},{3,2},{4,5},{5,4},{6,7},{7,6},{8,9},{9,8},{10,11... | collective-permute-start | bytes 5505032 | tf_op jit(solution)/shard_map/ppermute | solution.py:21
  79.0 1.8 %copy-start.1 = (bf16[2,4,4,8,7296]{4,3,2,1,0:T(8,128)(2,1)}, bf16[2,4,4,8,7296]{4,3,2,1,0:T(8,128)(2,1)S(1)}, u32[]{:S(2)}) copy-start(bf16[2,4,4,8,7296]{4,3,2,1,0:T(8,128)(2,1)S(1)} %pad_maximum_fusion.1) | copy-start | bytes 11206660
  95.4 2.6 %copy-start.3 = (bf16[256,7168]{1,0:T(8,128)(2,1)S(1)}, bf16[256,7168]{1,0:T(8,128)(2,1)}, u32[]{:S(2)}) copy-start(bf16[256,7168]{1,0:T(8,128)(2,1)} %fusion.5) | copy-start | bytes 11010052
  97.2 6.2 %collective-permute-start.23 = (bf16[128,7168]{1,0:T(8,128)(2,1)S(1)}, bf16[128,7168]{1,0:T(8,128)(2,1)S(1)}, u32[]{:S(2)}, u32[]{:S(2)}) collective-permute-start(bf16[128,7168]{1,0:T(8,128)(2,1)S(1)} %slice.139), channel_id=1, source_target_pairs={{0,1},{1,0},{2,3},{3,2},{4,5},{5,4},{6,7},{7,6},{8,9},{9,8},{10,11... | collective-permute-start | bytes 5505032 | tf_op jit(solution)/shard_map/ppermute | solution.py:21
  98.0 5.4 %copy-start.4 = (bf16[256,7168]{1,0:T(8,128)(2,1)S(1)}, bf16[256,7168]{1,0:T(8,128)(2,1)}, u32[]{:S(2)}) copy-start(bf16[256,7168]{1,0:T(8,128)(2,1)} %fusion.2) | copy-start | bytes 11010052
  100.3 8.9 %collective-permute-start.10 = (bf16[4,8,7168]{2,1,0:T(8,128)(2,1)S(1)}, bf16[4,8,7168]{2,1,0:T(8,128)(2,1)S(1)}, u32[]{:S(2)}, u32[]{:S(2)}) collective-permute-start(bf16[4,8,7168]{2,1,0:T(8,128)(2,1)S(1)} %get-tuple-element.18), channel_id=1, source_target_pairs={{0,4},{1,17},{2,6},{3,19},{4,8},{5,21},{6,10},{7,23},{8,12},{9,25}... | collective-permute-start | bytes 1376264 | tf_op jit(solution)/shard_map/ppermute | solution.py:21
  100.9 12.4 %collective-permute-start.8 = (bf16[4,8,7168]{2,1,0:T(8,128)(2,1)S(1)}, bf16[4,8,7168]{2,1,0:T(8,128)(2,1)S(1)}, u32[]{:S(2)}, u32[]{:S(2)}) collective-permute-start(bf16[4,8,7168]{2,1,0:T(8,128)(2,1)S(1)} %get-tuple-element.17), channel_id=1, source_target_pairs={{0,12},{1,49},{2,14},{3,51},{4,0},{5,53},{6,2},{7,55},{8,4},{9,57}... | collective-permute-start | bytes 1376264 | tf_op jit(solution)/shard_map/ppermute | solution.py:21
  103.1 11.4 %collective-permute-start.9 = (bf16[4,8,7168]{2,1,0:T(8,128)(2,1)S(1)}, bf16[4,8,7168]{2,1,0:T(8,128)(2,1)S(1)}, u32[]{:S(2)}, u32[]{:S(2)}) collective-permute-start(bf16[4,8,7168]{2,1,0:T(8,128)(2,1)S(1)} %get-tuple-element.19), channel_id=1, source_target_pairs={{0,8},{1,33},{2,10},{3,35},{4,12},{5,37},{6,14},{7,39},{8,0},{9,41... | collective-permute-start | bytes 1376264 | tf_op jit(solution)/shard_map/ppermute | solution.py:21
  103.9 19.8 %copy-start.5 = (bf16[1,8,7168]{2,1,0:T(8,128)(2,1)S(1)}, bf16[1,8,7168]{2,1,0:T(8,128)(2,1)}, u32[]{:S(2)}) copy-start(bf16[1,8,7168]{2,1,0:T(8,128)(2,1)} %param.6) | copy-start | bytes 344068
  114.7 5.9 %collective-permute-start.11 = (bf16[8,7168]{1,0:T(8,128)(2,1)S(1)}, bf16[8,7168]{1,0:T(8,128)(2,1)S(1)}, u32[]{:S(2)}, u32[]{:S(2)}) collective-permute-start(bf16[8,7168]{1,0:T(8,128)(2,1)S(1)} %get-tuple-element.31), channel_id=1, source_target_pairs={{0,48},{1,13},{2,50},{3,15},{4,52},{5,1},{6,54},{7,3},{8,56},{9,5}... | collective-permute-start | bytes 344072 | tf_op jit(solution)/shard_map/ppermute | solution.py:21
  117.1 5.2 %collective-permute-start.12 = (bf16[8,7168]{1,0:T(8,128)(2,1)S(1)}, bf16[8,7168]{1,0:T(8,128)(2,1)S(1)}, u32[]{:S(2)}, u32[]{:S(2)}) collective-permute-start(bf16[8,7168]{1,0:T(8,128)(2,1)S(1)} %get-tuple-element.33), channel_id=1, source_target_pairs={{0,32},{1,9},{2,34},{3,11},{4,36},{5,13},{6,38},{7,15},{8,40},{9,1... | collective-permute-start | bytes 344072 | tf_op jit(solution)/shard_map/ppermute | solution.py:21
  117.4 6.4 %collective-permute-start.13 = (bf16[8,7168]{1,0:T(8,128)(2,1)S(1)}, bf16[8,7168]{1,0:T(8,128)(2,1)S(1)}, u32[]{:S(2)}, u32[]{:S(2)}) collective-permute-start(bf16[8,7168]{1,0:T(8,128)(2,1)S(1)} %get-tuple-element.32), channel_id=1, source_target_pairs={{0,16},{1,5},{2,18},{3,7},{4,20},{5,9},{6,22},{7,11},{8,24},{9,13}... | collective-permute-start | bytes 344072 | tf_op jit(solution)/shard_map/ppermute | solution.py:21
  117.9 13.6 %collective-permute-start.24 = (bf16[4,8,7168]{2,1,0:T(8,128)(2,1)S(1)}, bf16[4,8,7168]{2,1,0:T(8,128)(2,1)S(1)}, u32[]{:S(2)}, u32[]{:S(2)}) collective-permute-start(bf16[4,8,7168]{2,1,0:T(8,128)(2,1)S(1)} %get-tuple-element.20), channel_id=1, source_target_pairs={{0,12},{1,49},{2,14},{3,51},{4,0},{5,53},{6,2},{7,55},{8,4},{9,57}... | collective-permute-start | bytes 1376264 | tf_op jit(solution)/shard_map/ppermute | solution.py:21
  120.3 11.2 %collective-permute-start.25 = (bf16[4,8,7168]{2,1,0:T(8,128)(2,1)S(1)}, bf16[4,8,7168]{2,1,0:T(8,128)(2,1)S(1)}, u32[]{:S(2)}, u32[]{:S(2)}) collective-permute-start(bf16[4,8,7168]{2,1,0:T(8,128)(2,1)S(1)} %get-tuple-element.22), channel_id=1, source_target_pairs={{0,8},{1,33},{2,10},{3,35},{4,12},{5,37},{6,14},{7,39},{8,0},{9,41... | collective-permute-start | bytes 1376264 | tf_op jit(solution)/shard_map/ppermute | solution.py:21
  120.7 14.9 %collective-permute-start.26 = (bf16[4,8,7168]{2,1,0:T(8,128)(2,1)S(1)}, bf16[4,8,7168]{2,1,0:T(8,128)(2,1)S(1)}, u32[]{:S(2)}, u32[]{:S(2)}) collective-permute-start(bf16[4,8,7168]{2,1,0:T(8,128)(2,1)S(1)} %get-tuple-element.21), channel_id=1, source_target_pairs={{0,4},{1,17},{2,6},{3,19},{4,8},{5,21},{6,10},{7,23},{8,12},{9,25}... | collective-permute-start | bytes 1376264 | tf_op jit(solution)/shard_map/ppermute | solution.py:21
  123.8 47.1 %collective-permute-start.14 = (f32[8,7168]{1,0:T(8,128)S(1)}, f32[8,7168]{1,0:T(8,128)S(1)}, u32[]{:S(2)}, u32[]{:S(2)}) collective-permute-start(f32[8,7168]{1,0:T(8,128)S(1)} %fusion.26), channel_id=1, source_target_pairs={{0,64},{1,65},{2,66},{3,67},{4,68},{5,69},{6,70},{7,71},{8,72},{9,... | collective-permute-start | bytes 688136 | tf_op jit(solution)/shard_map/ppermute | solution.py:123
  135.8 27.8 %collective-permute-start.27 = (bf16[8,7168]{1,0:T(8,128)(2,1)S(1)}, bf16[8,7168]{1,0:T(8,128)(2,1)S(1)}, u32[]{:S(2)}, u32[]{:S(2)}) collective-permute-start(bf16[8,7168]{1,0:T(8,128)(2,1)S(1)} %get-tuple-element.27), channel_id=1, source_target_pairs={{0,66},{1,67},{2,64},{3,65},{4,70},{5,71},{6,68},{7,69},{8,74},{9,... | collective-permute-start | bytes 344072 | tf_op jit(solution)/shard_map/ppermute | solution.py:131
  141.3 24.7 %collective-permute-start.28 = (bf16[8,7168]{1,0:T(8,128)(2,1)S(1)}, bf16[8,7168]{1,0:T(8,128)(2,1)S(1)}, u32[]{:S(2)}, u32[]{:S(2)}) collective-permute-start(bf16[8,7168]{1,0:T(8,128)(2,1)S(1)} %get-tuple-element.30), channel_id=1, source_target_pairs={{0,114},{1,79},{2,112},{3,77},{4,118},{5,67},{6,116},{7,65},{8,122... | collective-permute-start | bytes 344072 | tf_op jit(solution)/shard_map/ppermute | solution.py:131
  142.9 25.6 %collective-permute-start.29 = (bf16[8,7168]{1,0:T(8,128)(2,1)S(1)}, bf16[8,7168]{1,0:T(8,128)(2,1)S(1)}, u32[]{:S(2)}, u32[]{:S(2)}) collective-permute-start(bf16[8,7168]{1,0:T(8,128)(2,1)S(1)} %get-tuple-element.29), channel_id=1, source_target_pairs={{0,98},{1,75},{2,96},{3,73},{4,102},{5,79},{6,100},{7,77},{8,106},... | collective-permute-start | bytes 344072 | tf_op jit(solution)/shard_map/ppermute | solution.py:131
  146.8 24.2 %collective-permute-start.30 = (bf16[8,7168]{1,0:T(8,128)(2,1)S(1)}, bf16[8,7168]{1,0:T(8,128)(2,1)S(1)}, u32[]{:S(2)}, u32[]{:S(2)}) collective-permute-start(bf16[8,7168]{1,0:T(8,128)(2,1)S(1)} %get-tuple-element.28), channel_id=1, source_target_pairs={{0,82},{1,71},{2,80},{3,69},{4,86},{5,75},{6,84},{7,73},{8,90},{9,... | collective-permute-start | bytes 344072 | tf_op jit(solution)/shard_map/ppermute | solution.py:131
